TPU v7x, 256 devices: a whole 4x4x8 slice. The times are simulated.
256 devices in a mesh: section: 4 (over x), expert: 64 (over y, z, core).
Axes of the slice: x: 4, y: 4, z: 8, core: 2. Of those that a mesh axis runs over, the one named last changes fastest.
Arguments:
- acts: bfloat16 [4, 2, 4096, 3584], P('section', None, 'expert'), may hold values from -6 to 6
- norm_gain: float32 [4, 3584], P('section'), may hold values from 0.1 to 1.9
- router: bfloat16 [4, 3584, 16], P('section'), may hold values from -0.09375 to 0.09375
- routes: int32 [4, 2, 2, 4096, 1], P('section', None, None, 'expert'), may hold values from 0 to 15; in each aligned block of 64 rows (0 to 63, 64 to 127, ..., all dimensions but the last counted through in order) at most 8 rows name the same one
- w_gate: bfloat16 [4, 64, 3584, 256], P('section', 'expert'), may hold values from -0.09375 to 0.09375
- w_up: bfloat16 [4, 64, 3584, 256], P('section', 'expert'), may hold values from -0.09375 to 0.09375
- w_down: bfloat16 [4, 64, 256, 3584], P('section', 'expert'), may hold values from -0.375 to 0.375
Outputs:
- finished: bfloat16 [4, 2, 4096, 3584], P('section', None, 'expert')
Inputs may be any that keep to these rules, and one draw needn't show every extreme that they name: `routes`: within each block of 64 tokens of one device, for each layer, round and micro-batch, no expert is named by more than 8 tokens, a bound that some block reaches.
All inputs are finite; a program needn't handle non-finite values.
Results may differ from a plain program's by a relative error of at most 0.0072.
Values may be sent and summed in bfloat16 or wider, within the bound.
No kernel may reach another device: no remote copies, remote signals or barrier semaphores. Data moves between devices by JAX's collectives and lax.ppermute only.
A program may use at most 128 MiB of HBM per device.

v0:
```python
import jax
import jax.numpy as jnp
from jax import lax
from jax.sharding import PartitionSpec as P


def for_sending(shard):

    def short(part):
        return part.astype(jnp.bfloat16) if part.dtype == jnp.float32 else part

    return jax.tree.map(short, shard)


def passed_along(value, axis, steps):
    count = lax.axis_size(axis)
    pairs = [(source, (source + steps) % count) for source in range(count)]
    return lax.ppermute(value, axis, pairs)


def body(acts, norm_gain, router, routes, w_gate, w_up, w_down):
    devices = lax.axis_size("expert")
    experts_here = router.shape[2]
    group_size = devices // experts_here
    tok_local = acts.shape[2]
    width = acts.shape[3]
    capacity = 2 * tok_local // experts_here
    gain_row = norm_gain[0]
    router_mat = router[0]
    gate_mat = w_gate[0, 0]
    up_mat = w_up[0, 0]
    down_mat = w_down[0, 0]

    def expert_compute(rows_box):
        count = rows_box.shape[1]
        rows_in = rows_box.reshape(devices * count, width)
        gate_proj = jnp.dot(rows_in, gate_mat, preferred_element_type=jnp.float32)
        up_proj = jnp.dot(rows_in, up_mat, preferred_element_type=jnp.float32)
        hidden = (jax.nn.silu(gate_proj) * up_proj).astype(jnp.bfloat16)
        partial_out = jnp.dot(hidden, down_mat, preferred_element_type=jnp.float32).astype(
            jnp.bfloat16
        )
        return partial_out.reshape(devices, count, width)

    def expert_work(rows_box):
        return lax.all_to_all(
            expert_compute(rows_box), "expert", split_axis=0, concat_axis=0, tiled=True
        )

    def apply_layer(tokens_in, route_ids):
        x_float = tokens_in.astype(jnp.float32)
        mean_sq = jnp.mean(x_float * x_float, axis=1, keepdims=True)
        normed = (x_float * lax.rsqrt(mean_sq + 1e-06) * gain_row[None, :]).astype(jnp.bfloat16)
        scores = jnp.dot(normed, router_mat, preferred_element_type=jnp.float32)
        chosen = route_ids[:, 0]
        onehot = (chosen[:, None] == jnp.arange(experts_here, dtype=jnp.int32)[None, :]).astype(
            jnp.int32
        )
        gate_val = jax.nn.sigmoid(jnp.sum(scores * onehot.astype(jnp.float32), axis=1))
        slot_of = jnp.sum(jnp.cumsum(onehot, axis=0) * onehot, axis=1) - 1
        flat_slot = chosen * capacity + slot_of
        placing = (
            flat_slot[None, :] == jnp.arange(experts_here * capacity, dtype=jnp.int32)[:, None]
        ).astype(jnp.bfloat16)
        outbox = jnp.dot(placing, normed, preferred_element_type=jnp.float32).astype(jnp.bfloat16)
        outbox = outbox.reshape(experts_here, capacity, width)
        sendout = jnp.broadcast_to(outbox[None], (group_size, experts_here, capacity, width))
        sendout = sendout.reshape(devices, capacity, width)
        returned = expert_work(
            lax.all_to_all(sendout, "expert", split_axis=0, concat_axis=0, tiled=True)
        )
        combined = jnp.sum(
            returned.reshape(group_size, experts_here, capacity, width).astype(jnp.float32), axis=0
        )
        combined = combined.reshape(experts_here * capacity, width)
        picked = jnp.take(combined, flat_slot, axis=0)
        return (x_float + gate_val[:, None] * picked).astype(jnp.bfloat16)

    micro_count = acts.shape[1]
    carried = [acts[0, micro_idx] for micro_idx in range(micro_count)]
    for round_idx in range(routes.shape[1]):
        updated_all = [
            apply_layer(carried[micro_idx], routes[0, round_idx, micro_idx])
            for micro_idx in range(micro_count)
        ]
        carried = list(passed_along(for_sending(tuple(updated_all)), "section", 1))
    return jnp.stack(carried)[None]


def solution(mesh):
    in_specs = (
        P("section", None, "expert", None),
        P("section", None),
        P("section", None, None),
        P("section", None, None, "expert", None),
        P("section", "expert", None, None),
        P("section", "expert", None, None),
        P("section", "expert", None, None),
    )
    out_specs = P("section", None, "expert", None)
    return jax.shard_map(body, mesh=mesh, in_specs=in_specs, out_specs=out_specs, check_vma=False)
```

profile of v0, /device:TPU:1, one launch (start us, length us, event | category | flops | bytes accessed | tf_op | source)
XLA Modules:
  0.0 799.9 jit_solution(8249525880172718764)
XLA Ops:
  0.0 1.6 fusion.86
  4.9 1.5 fusion.4
  6.4 2.1 broadcast_in_dim.28
  8.5 13.4 %all-to-all-start = ((bf16[64,8,3584]{2,1,0:T(8,128)(2,1)}), bf16[64,8,3584]{2,1,0:T(8,128)(2,1)}, u32[]{:S(2)}, u32[]{:S(2)}) async-start(bf16[64,8,3584]{2,1,0:T(8,128)(2,1)} %bitcast.207), calls=%async_computation | async-start | bytes 7340032 | tf_op jit(solution)/shard_map/all_to_all | solution.py:70
  22.0 1.4 fusion.6
  23.3 83.2 %all-to-all-done = bf16[64,8,3584]{2,1,0:T(8,128)(2,1)} async-done(((bf16[64,8,3584]{2,1,0:T(8,128)(2,1)}), bf16[64,8,3584]{2,1,0:T(8,128)(2,1)}, u32[]{:S(2)}, u32[]{:S(2)}) %all-to-all-start) | async-done | bytes 3670048 | tf_op jit(solution)/shard_map/all_to_all | solution.py:70
  106.6 3.4 broadcast_in_dim.32
  110.0 5.9 all-to-all-start.4
  115.9 4.5 fusion.22
  120.4 8.5 %fusion = bf16[64,8,3584]{2,1,0:T(8,128)(2,1)} fusion(bf16[1,1,256,3584]{3,2,1,0:T(8,128)(2,1)S(1)} %copy-done, bf16[1,1,3584,256]{3,2,1,0:T(8,128)(2,1)} %param.14, bf16[64,8,3584]{2,1,0:T(8,128)(2,1)} %all-to-all-done, f32[512,256]{1,0:T(8,128)} %fusion.22), kind=kOutput, calls=%fused_computation.12 | convolution fusion | flops 1881669632 | bytes 11534336 | tf_op jit(solution)/shard_map/dot_general | solution.py:40
  128.9 71.6 %all-to-all-done.4 = bf16[64,8,3584]{2,1,0:T(8,128)(2,1)} async-done(((bf16[64,8,3584]{2,1,0:T(8,128)(2,1)}), bf16[64,8,3584]{2,1,0:T(8,128)(2,1)}, u32[]{:S(2)}, u32[]{:S(2)}) %all-to-all-start.4) | async-done | bytes 3670048 | tf_op jit(solution)/shard_map/all_to_all | solution.py:70
  200.5 5.9 all-to-all-start.1
  206.4 4.5 fusion.14
  211.0 8.5 %fusion.2 = bf16[64,8,3584]{2,1,0:T(8,128)(2,1)} fusion(bf16[1,1,256,3584]{3,2,1,0:T(8,128)(2,1)S(1)} %copy-done, bf16[1,1,3584,256]{3,2,1,0:T(8,128)(2,1)} %param.14, bf16[64,8,3584]{2,1,0:T(8,128)(2,1)} %all-to-all-done.4, f32[512,256]{1,0:T(8,128)} %fusion.14), kind=kOutput, calls=%fused_computation.14 | convolution fusion | flops 1881669632 | bytes 11534336 | tf_op jit(solution)/shard_map/dot_general | solution.py:40
  219.5 71.6 %all-to-all-done.1 = bf16[64,8,3584]{2,1,0:T(8,128)(2,1)} async-done(((bf16[64,8,3584]{2,1,0:T(8,128)(2,1)}), bf16[64,8,3584]{2,1,0:T(8,128)(2,1)}, u32[]{:S(2)}, u32[]{:S(2)}) %all-to-all-start.1) | async-done | bytes 3670048 | tf_op jit(solution)/shard_map/all_to_all | solution.py:46
  291.1 6.1 all-to-all-start.5
  297.9 4.1 convert_reduce_fusion.3
  302.0 79.8 %all-to-all-done.5 = bf16[64,8,3584]{2,1,0:T(8,128)(2,1)} async-done(((bf16[64,8,3584]{2,1,0:T(8,128)(2,1)}), bf16[64,8,3584]{2,1,0:T(8,128)(2,1)}, u32[]{:S(2)}, u32[]{:S(2)}) %all-to-all-start.5) | async-done | bytes 3670048 | tf_op jit(solution)/shard_map/all_to_all | solution.py:46
  381.8 4.0 convert_reduce_fusion.1
  385.8 3.7 gather_fusion
  389.5 3.7 gather_fusion.2
  393.2 1.8 fusion.89
  395.0 1.3 collective-permute-start.2
  396.2 11.7 %collective-permute-done.2 = bf16[64,3584]{1,0:T(8,128)(2,1)S(1)} collective-permute-done((bf16[64,3584]{1,0:T(8,128)(2,1)S(1)}, bf16[64,3584]{1,0:T(8,128)(2,1)S(1)}, u32[]{:S(2)}, u32[]{:S(2)}) %collective-permute-start.2) | collective-permute-done | bytes 458784 | tf_op jit(solution)/shard_map/ppermute | solution.py:18
  408.7 2.1 broadcast_in_dim.34
  410.8 6.2 all-to-all-start.6
  417.1 12.7 %collective-permute-done = bf16[64,3584]{1,0:T(8,128)(2,1)S(1)} collective-permute-done((bf16[64,3584]{1,0:T(8,128)(2,1)S(1)}, bf16[64,3584]{1,0:T(8,128)(2,1)S(1)}, u32[]{:S(2)}, u32[]{:S(2)}) %collective-permute-start) | collective-permute-done | bytes 458784 | tf_op jit(solution)/shard_map/ppermute | solution.py:18
  430.0 1.4 fusion.5
  431.4 70.3 %all-to-all-done.6 = bf16[64,8,3584]{2,1,0:T(8,128)(2,1)} async-done(((bf16[64,8,3584]{2,1,0:T(8,128)(2,1)}), bf16[64,8,3584]{2,1,0:T(8,128)(2,1)}, u32[]{:S(2)}, u32[]{:S(2)}) %all-to-all-start.6) | async-done | bytes 3670048 | tf_op jit(solution)/shard_map/all_to_all | solution.py:70
  501.7 3.4 broadcast_in_dim.30
  505.0 6.0 all-to-all-start.2
  511.0 4.5 fusion.10
  515.5 8.5 %fusion.3 = bf16[64,8,3584]{2,1,0:T(8,128)(2,1)} fusion(bf16[1,1,256,3584]{3,2,1,0:T(8,128)(2,1)S(1)} %copy-done, bf16[1,1,3584,256]{3,2,1,0:T(8,128)(2,1)} %param.14, bf16[64,8,3584]{2,1,0:T(8,128)(2,1)} %all-to-all-done.6, f32[512,256]{1,0:T(8,128)} %fusion.10), kind=kOutput, calls=%fused_computation.15 | convolution fusion | flops 1881669632 | bytes 11534336 | tf_op jit(solution)/shard_map/dot_general | solution.py:40
  524.1 71.6 %all-to-all-done.2 = bf16[64,8,3584]{2,1,0:T(8,128)(2,1)} async-done(((bf16[64,8,3584]{2,1,0:T(8,128)(2,1)}), bf16[64,8,3584]{2,1,0:T(8,128)(2,1)}, u32[]{:S(2)}, u32[]{:S(2)}) %all-to-all-start.2) | async-done | bytes 3670048 | tf_op jit(solution)/shard_map/all_to_all | solution.py:70
  595.7 5.9 all-to-all-start.7
  601.6 4.5 fusion.18
  606.1 8.4 %fusion.1 = bf16[64,8,3584]{2,1,0:T(8,128)(2,1)} fusion(bf16[1,1,256,3584]{3,2,1,0:T(8,128)(2,1)S(1)} %copy-done, bf16[1,1,3584,256]{3,2,1,0:T(8,128)(2,1)} %param.14, bf16[64,8,3584]{2,1,0:T(8,128)(2,1)} %all-to-all-done.2, f32[512,256]{1,0:T(8,128)} %fusion.18), kind=kOutput, calls=%fused_computation.13 | convolution fusion | flops 1881669632 | bytes 11534336 | tf_op jit(solution)/shard_map/dot_general | solution.py:40
  614.5 71.7 %all-to-all-done.7 = bf16[64,8,3584]{2,1,0:T(8,128)(2,1)} async-done(((bf16[64,8,3584]{2,1,0:T(8,128)(2,1)}), bf16[64,8,3584]{2,1,0:T(8,128)(2,1)}, u32[]{:S(2)}, u32[]{:S(2)}) %all-to-all-start.7) | async-done | bytes 3670048 | tf_op jit(solution)/shard_map/all_to_all | solution.py:46
  686.2 5.9 all-to-all-start.3
  692.8 4.0 convert_reduce_fusion
  696.8 3.7 gather_fusion.3
  700.5 1.4 fusion.105
  702.3 74.5 %all-to-all-done.3 = bf16[64,8,3584]{2,1,0:T(8,128)(2,1)} async-done(((bf16[64,8,3584]{2,1,0:T(8,128)(2,1)}), bf16[64,8,3584]{2,1,0:T(8,128)(2,1)}, u32[]{:S(2)}, u32[]{:S(2)}) %all-to-all-start.3) | async-done | bytes 3670048 | tf_op jit(solution)/shard_map/all_to_all | solution.py:46
  776.8 4.0 convert_reduce_fusion.2
  780.8 3.7 gather_fusion.1
  784.4 1.4 fusion.101
  785.9 12.9 %collective-permute-done.1 = bf16[64,3584]{1,0:T(8,128)(2,1)S(1)} collective-permute-done((bf16[64,3584]{1,0:T(8,128)(2,1)S(1)}, bf16[64,3584]{1,0:T(8,128)(2,1)S(1)}, u32[]{:S(2)}, u32[]{:S(2)}) %collective-permute-start.1) | collective-permute-done | bytes 458784 | tf_op jit(solution)/shard_map/ppermute | solution.py:18
  798.9 1.0 maximum_bitcast_fusion
  (53 shorter events, 6.0 us)
Async XLA Ops:
  0.0 120.4 %copy-start = (bf16[1,1,256,3584]{3,2,1,0:T(8,128)(2,1)S(1)}, bf16[1,1,256,3584]{3,2,1,0:T(8,128)(2,1)}, u32[]{:S(2)}) copy-start(bf16[1,1,256,3584]{3,2,1,0:T(8,128)(2,1)} %param.15) | copy-start | bytes 5505028
  8.5 13.5 %copy-start.1 = (bf16[1,2,64,3584]{3,2,1,0:T(8,128)(2,1)S(1)}, bf16[1,2,64,3584]{3,2,1,0:T(8,128)(2,1)}, u32[]{:S(2)}) copy-start(bf16[1,2,64,3584]{3,2,1,0:T(8,128)(2,1)} %param.9) | copy-start | bytes 2752516
  8.5 98.1 %all-to-all-start = ((bf16[64,8,3584]{2,1,0:T(8,128)(2,1)}), bf16[64,8,3584]{2,1,0:T(8,128)(2,1)}, u32[]{:S(2)}, u32[]{:S(2)}) async-start(bf16[64,8,3584]{2,1,0:T(8,128)(2,1)} %bitcast.207), calls=%async_computation | async-start | bytes 7340032 | tf_op jit(solution)/shard_map/all_to_all | solution.py:70
  110.0 90.6 %all-to-all-start.4 = ((bf16[64,8,3584]{2,1,0:T(8,128)(2,1)}), bf16[64,8,3584]{2,1,0:T(8,128)(2,1)}, u32[]{:S(2)}, u32[]{:S(2)}) async-start(bf16[64,8,3584]{2,1,0:T(8,128)(2,1)} %bitcast.205), calls=%async_computation.4 | async-start | bytes 7340032 | tf_op jit(solution)/shard_map/all_to_all | solution.py:70
  200.5 90.6 %all-to-all-start.1 = ((bf16[64,8,3584]{2,1,0:T(8,128)(2,1)}), bf16[64,8,3584]{2,1,0:T(8,128)(2,1)}, u32[]{:S(2)}, u32[]{:S(2)}) async-start(bf16[64,8,3584]{2,1,0:T(8,128)(2,1)} %fusion), calls=%async_computation.1 | async-start | bytes 7340032 | tf_op jit(solution)/shard_map/all_to_all | solution.py:46
  219.5 77.8 %copy-start.2 = (bf16[1,3584,16]{1,2,0:T(8,128)(2,1)S(1)}, bf16[1,3584,16]{1,2,0:T(8,128)(2,1)}, u32[]{:S(2)}) copy-start(bf16[1,3584,16]{1,2,0:T(8,128)(2,1)} %param.11) | copy-start | bytes 344068
  291.1 90.7 %all-to-all-start.5 = ((bf16[64,8,3584]{2,1,0:T(8,128)(2,1)}), bf16[64,8,3584]{2,1,0:T(8,128)(2,1)}, u32[]{:S(2)}, u32[]{:S(2)}) async-start(bf16[64,8,3584]{2,1,0:T(8,128)(2,1)} %fusion.2), calls=%async_computation.5 | async-start | bytes 7340032 | tf_op jit(solution)/shard_map/all_to_all | solution.py:46
  395.0 13.0 %collective-permute-start.2 = (bf16[64,3584]{1,0:T(8,128)(2,1)S(1)}, bf16[64,3584]{1,0:T(8,128)(2,1)S(1)}, u32[]{:S(2)}, u32[]{:S(2)}) collective-permute-start(bf16[64,3584]{1,0:T(8,128)(2,1)S(1)} %get-tuple-element.17), channel_id=1, source_target_pairs={{0,64},{64,128},{128,192},{192,0},{1,65},{65,129},{129,193},{193,1... | collective-permute-start | bytes 1376264 | tf_op jit(solution)/shard_map/ppermute | solution.py:18
  410.8 90.9 %all-to-all-start.6 = ((bf16[64,8,3584]{2,1,0:T(8,128)(2,1)}), bf16[64,8,3584]{2,1,0:T(8,128)(2,1)}, u32[]{:S(2)}, u32[]{:S(2)}) async-start(bf16[64,8,3584]{2,1,0:T(8,128)(2,1)} %bitcast.204), calls=%async_computation.6 | async-start | bytes 7340032 | tf_op jit(solution)/shard_map/all_to_all | solution.py:70
  417.0 12.8 %collective-permute-start = (bf16[64,3584]{1,0:T(8,128)(2,1)S(1)}, bf16[64,3584]{1,0:T(8,128)(2,1)S(1)}, u32[]{:S(2)}, u32[]{:S(2)}) collective-permute-start(bf16[64,3584]{1,0:T(8,128)(2,1)S(1)} %get-tuple-element.16), channel_id=1, source_target_pairs={{0,64},{64,128},{128,192},{192,0},{1,65},{65,129},{129,193},{193,1... | collective-permute-start | bytes 1376264 | tf_op jit(solution)/shard_map/ppermute | solution.py:18
  505.0 90.6 %all-to-all-start.2 = ((bf16[64,8,3584]{2,1,0:T(8,128)(2,1)}), bf16[64,8,3584]{2,1,0:T(8,128)(2,1)}, u32[]{:S(2)}, u32[]{:S(2)}) async-start(bf16[64,8,3584]{2,1,0:T(8,128)(2,1)} %bitcast.206), calls=%async_computation.2 | async-start | bytes 7340032 | tf_op jit(solution)/shard_map/all_to_all | solution.py:70
  595.7 90.6 %all-to-all-start.7 = ((bf16[64,8,3584]{2,1,0:T(8,128)(2,1)}), bf16[64,8,3584]{2,1,0:T(8,128)(2,1)}, u32[]{:S(2)}, u32[]{:S(2)}) async-start(bf16[64,8,3584]{2,1,0:T(8,128)(2,1)} %fusion.3), calls=%async_computation.7 | async-start | bytes 7340032 | tf_op jit(solution)/shard_map/all_to_all | solution.py:46
  686.2 90.6 %all-to-all-start.3 = ((bf16[64,8,3584]{2,1,0:T(8,128)(2,1)}), bf16[64,8,3584]{2,1,0:T(8,128)(2,1)}, u32[]{:S(2)}, u32[]{:S(2)}) async-start(bf16[64,8,3584]{2,1,0:T(8,128)(2,1)} %fusion.1), calls=%async_computation.3 | async-start | bytes 7340032 | tf_op jit(solution)/shard_map/all_to_all | solution.py:46
  701.9 84.0 %collective-permute-start.3 = (bf16[64,3584]{1,0:T(8,128)(2,1)S(1)}, bf16[64,3584]{1,0:T(8,128)(2,1)S(1)}, u32[]{:S(2)}, u32[]{:S(2)}) collective-permute-start(bf16[64,3584]{1,0:T(8,128)(2,1)S(1)} %fusion.105), channel_id=1, source_target_pairs={{0,64},{64,128},{128,192},{192,0},{1,65},{65,129},{129,193},{193,1... | collective-permute-start | bytes 1376264 | tf_op jit(solution)/shard_map/ppermute | solution.py:18
  785.8 13.0 %collective-permute-start.1 = (bf16[64,3584]{1,0:T(8,128)(2,1)S(1)}, bf16[64,3584]{1,0:T(8,128)(2,1)S(1)}, u32[]{:S(2)}, u32[]{:S(2)}) collective-permute-start(bf16[64,3584]{1,0:T(8,128)(2,1)S(1)} %fusion.101), channel_id=1, source_target_pairs={{0,64},{64,128},{128,192},{192,0},{1,65},{65,129},{129,193},{193,1... | collective-permute-start | bytes 1376264 | tf_op jit(solution)/shard_map/ppermute | solution.py:18
where the time goes:
time: 801 us; the launch traced here: 800 us
  waiting for transfers between devices  632 us (79%)
  matrix products  58 us (7%)
  starting transfers between devices  57.1 us (7%)
  local copies, waits for them, and re-layouts  27 us (3%)
  other arithmetic  25.6 us (3%)
    all_to_all x4, waiting for transfers between devices, expert_work(): lax.all_to_all(expert_compute(rows_box), 'expert', split_axis=0, concat_a...  298 us
    all_to_all x4, waiting for transfers between devices, apply_layer(): lax.all_to_all(sendout, 'expert', split_axis=0, concat_axis=0, tiled=True)  297 us
    ppermute x4, waiting for transfers between devices, passed_along(): return lax.ppermute(value, axis, pairs)  37.4 us
    dot_general x4, matrix products, expert_compute(): jnp.dot(hidden, down_mat, preferred_element_type=jnp.float32)  34 us
    all_to_all x4, starting transfers between devices, apply_layer(): lax.all_to_all(sendout, 'expert', split_axis=0, concat_axis=0, tiled=True)  31.5 us
    all_to_all x4, starting transfers between devices, expert_work(): lax.all_to_all(expert_compute(rows_box), 'expert', split_axis=0, concat_a...  23.8 us
    dot_general x4, matrix products, expert_compute(): gate_proj = jnp.dot(rows_in, gate_mat, preferred_element_type=jnp.float32)  18.1 us
    reduce_sum x4, other arithmetic, apply_layer(): jnp.sum(returned.reshape(group_size, experts_here, capacity, width).astyp...  16.1 us
  transfers between devices with their start and end apart: 12, of which 11 were waited for; matrix products, arithmetic and copies ran while one was open for 10% of the time, Pallas kernels for 0%

commit v1 on v0

v1 whole, which is shorter than its diff:
```python
import jax
import jax.numpy as jnp
from jax import lax
from jax.sharding import Mesh
from jax.sharding import PartitionSpec as P

ROW = ("z", "core")
EXP = ("y", "z", "core")


def passed_along(value, axis, steps):
    count = lax.axis_size(axis)
    pairs = [(source, (source + steps) % count) for source in range(count)]
    return lax.ppermute(value, axis, pairs)


def body(acts, norm_gain, router, routes, w_gate, w_up, w_down):
    experts_here = router.shape[2]
    row_size = lax.axis_size("z") * lax.axis_size("core")
    tok_local = acts.shape[2]
    width = acts.shape[3]
    capacity = 2 * tok_local // experts_here
    gain_row = norm_gain[0]
    router_mat = router[0]
    gate_mat = w_gate[0, 0]
    up_mat = w_up[0, 0]
    down_mat = w_down[0, 0]

    def expert_compute(rows_in):
        gate_proj = jnp.dot(rows_in, gate_mat, preferred_element_type=jnp.float32)
        up_proj = jnp.dot(rows_in, up_mat, preferred_element_type=jnp.float32)
        hidden = (jax.nn.silu(gate_proj) * up_proj).astype(jnp.bfloat16)
        return jnp.dot(hidden, down_mat, preferred_element_type=jnp.float32).astype(jnp.bfloat16)

    def apply_layer(tokens_in, route_ids):
        x_float = tokens_in.astype(jnp.float32)
        mean_sq = jnp.mean(x_float * x_float, axis=1, keepdims=True)
        normed = (x_float * lax.rsqrt(mean_sq + 1e-06) * gain_row[None, :]).astype(jnp.bfloat16)
        scores = jnp.dot(normed, router_mat, preferred_element_type=jnp.float32)
        chosen = route_ids[:, 0]
        onehot = (chosen[:, None] == jnp.arange(experts_here, dtype=jnp.int32)[None, :]).astype(
            jnp.int32
        )
        gate_val = jax.nn.sigmoid(jnp.sum(scores * onehot.astype(jnp.float32), axis=1))
        slot_of = jnp.sum(jnp.cumsum(onehot, axis=0) * onehot, axis=1) - 1
        flat_slot = chosen * capacity + slot_of
        placing = (
            flat_slot[None, :] == jnp.arange(experts_here * capacity, dtype=jnp.int32)[:, None]
        ).astype(jnp.bfloat16)
        outbox = jnp.dot(placing, normed, preferred_element_type=jnp.float32).astype(jnp.bfloat16)
        outbox = outbox.reshape(row_size, capacity, width)
        arrived = lax.all_to_all(outbox, ROW, split_axis=0, concat_axis=0, tiled=True)
        rows = lax.all_gather(arrived, "y", axis=0, tiled=True)
        partial_out = expert_compute(rows.reshape(-1, width))
        summed = lax.psum_scatter(partial_out, "y", scatter_dimension=0, tiled=True)
        back = lax.all_to_all(
            summed.reshape(row_size, capacity, width), ROW, split_axis=0, concat_axis=0, tiled=True
        )
        picked = jnp.dot(
            placing.T, back.reshape(experts_here * capacity, width), preferred_element_type=jnp.float32
        )
        return (x_float + gate_val[:, None] * picked).astype(jnp.bfloat16)

    micro_count = acts.shape[1]
    carried = [acts[0, micro_idx] for micro_idx in range(micro_count)]
    for round_idx in range(routes.shape[1]):
        carried = [
            passed_along(apply_layer(carried[micro_idx], routes[0, round_idx, micro_idx]), "section", 1)
            for micro_idx in range(micro_count)
        ]
    return jnp.stack(carried)[None]


def solution(mesh):
    n_sec, n_exp = mesh.devices.shape
    n_core = 2
    n_y = n_exp // (n_core * 8)
    grid = mesh.devices.reshape(n_sec, n_y, n_exp // (n_y * n_core), n_core)
    fine = Mesh(grid, ("section", "y", "z", "core"))
    in_specs = (
        P("section", None, EXP, None),
        P("section", None),
        P("section", None, None),
        P("section", None, None, EXP, None),
        P("section", EXP, None, None),
        P("section", EXP, None, None),
        P("section", EXP, None, None),
    )
    out_specs = P("section", None, EXP, None)
    return jax.shard_map(body, mesh=fine, in_specs=in_specs, out_specs=out_specs, check_vma=False)
```

time: 801 us -> 529 us (0.66)
  waiting for transfers between devices: 632 us -> 289 us
  blocking collectives: 0 us -> 125 us
  local copies, waits for them, and re-layouts: 27 us -> 1.31 us
  starting transfers between devices: 57.1 us -> 31.8 us
  other arithmetic: 25.6 us -> 4.99 us
  between operations: 0.28 us -> 13.7 us
    all_to_all x8 -> x4, waiting for transfers between devices: 594 us -> 70.1 us  [apply_layer(): lax.all_to_all(summed.reshape(row_size, capacity, width), ROW, split_axis...]
    all_to_all x0 -> x4, blocking collectives: none -> 125 us  [apply_layer(): lax.all_to_all(outbox, ROW, split_axis=0, concat_axis=0, tiled=True)]
    reduce_scatter x0 -> x4, waiting for transfers between devices: none -> 110 us  [apply_layer(): summed = lax.psum_scatter(partial_out, 'y', scatter_dimension=0, tiled=True)]
    all_gather x0 -> x4, waiting for transfers between devices: none -> 74.9 us  [apply_layer(): rows = lax.all_gather(arrived, 'y', axis=0, tiled=True)]
    all_to_all x8 -> x4, starting transfers between devices: 55.3 us -> 27.6 us  [apply_layer(): lax.all_to_all(summed.reshape(row_size, capacity, width), ROW, split_axis...]
    reduce_sum x4 -> x0, other arithmetic: 16.1 us -> none  [apply_layer(): jnp.sum(returned.reshape(group_size, experts_here, capacity, width).astyp...]
    gather x4 -> x0, local copies, waits for them, and re-layouts: 14.7 us -> none  [apply_layer(): picked = jnp.take(combined, flat_slot, axis=0)]
    broadcast_in_dim x4 -> x0, local copies, waits for them, and re-layouts: 11 us -> none  [apply_layer(): jnp.broadcast_to(outbox[None], (group_size, experts_here, capacity, width))]
  transfers between devices with their start and end apart: 12 -> 16, of which waited for: 11 -> 12; matrix products, arithmetic and copies ran while one was open for 10% -> 12% of each run, Pallas kernels for 0% -> 0%
where the time goes in v1:
time: 529 us; the launch traced here: 528 us
  waiting for transfers between devices  289 us (55%)
  blocking collectives  125 us (24%)
  matrix products  62.4 us (12%)
  starting transfers between devices  31.8 us (6%)
  between operations  13.7 us (3%)
    all_to_all x4, blocking collectives, apply_layer(): lax.all_to_all(outbox, ROW, split_axis=0, concat_axis=0, tiled=True)  125 us
    reduce_scatter x4, waiting for transfers between devices, apply_layer(): summed = lax.psum_scatter(partial_out, 'y', scatter_dimension=0, tiled=True)  110 us
    all_gather x4, waiting for transfers between devices, apply_layer(): rows = lax.all_gather(arrived, 'y', axis=0, tiled=True)  74.9 us
    all_to_all x4, waiting for transfers between devices, apply_layer(): lax.all_to_all(summed.reshape(row_size, capacity, width), ROW, split_axis...  70.1 us
    dot_general x4, matrix products, expert_compute(): jnp.dot(hidden, down_mat, preferred_element_type=jnp.float32)  34.3 us
    ppermute x4, waiting for transfers between devices, passed_along(): return lax.ppermute(value, axis, pairs)  33.7 us
    all_to_all x4, starting transfers between devices, apply_layer(): lax.all_to_all(summed.reshape(row_size, capacity, width), ROW, split_axis...  27.6 us
    dot_general x4, matrix products, expert_compute(): gate_proj = jnp.dot(rows_in, gate_mat, preferred_element_type=jnp.float32)  18.1 us
  transfers between devices with their start and end apart: 16, of which 12 were waited for; matrix products, arithmetic and copies ran while one was open for 12% of the time, Pallas kernels for 0%

profile of v1, /device:TPU:1, one launch (start us, length us, event | category | flops | bytes accessed | tf_op | source)
XLA Modules:
  0.0 528.2 jit_solution(9062437544798600943)
XLA Ops:
  6.5 1.6 fusion.104
  8.1 0.7 slice_bitcast_fusion.2
  9.9 0.8 reduce
  10.7 0.7 add_add_fusion.2
  11.4 0.5 fusion.6
  11.9 35.5 %all_to_all.40 = bf16[16,8,3584]{2,1,0:T(8,128)(2,1)} all-to-all(bf16[16,8,3584]{2,1,0:T(8,128)(2,1)S(1)} %fusion.6), channel_id=1, replica_groups=mesh['section'=4,'y'=4,'z'=8,'core'=2] {'z','core'}, dimensions={0} | all-to-all | bytes 1835008 | tf_op jit(solution)/shard_map/all_to_all | solution.py:52
  47.5 0.5 fusion.4
  48.0 28.5 %all_to_all.41 = bf16[16,8,3584]{2,1,0:T(8,128)(2,1)} all-to-all(bf16[16,8,3584]{2,1,0:T(8,128)(2,1)S(1)} %fusion.4), channel_id=1, replica_groups=mesh['section'=4,'y'=4,'z'=8,'core'=2] {'z','core'}, dimensions={0} | all-to-all | bytes 1835008 | tf_op jit(solution)/shard_map/all_to_all | solution.py:52
  76.5 14.1 %all-gather.9.cloned.1.call-done = bf16[64,8,3584]{2,1,0:T(8,128)(2,1)} async-done(((bf16[16,8,3584]{2,1,0:T(8,128)(2,1)}), bf16[64,8,3584]{2,1,0:T(8,128)(2,1)}) %all-gather.9.cloned.1.call-update) | async-done | bytes 3670032 | tf_op jit(solution)/shard_map/all_gather | solution.py:53
  90.6 4.5 fusion.18
  95.2 8.5 %convolution_convert_fusion.1 = bf16[512,3584]{1,0:T(8,128)(2,1)} fusion(bf16[1,1,256,3584]{3,2,1,0:T(8,128)(2,1)S(1)} %copy-done, bf16[1,1,3584,256]{3,2,1,0:T(8,128)(2,1)} %param.12, bf16[64,8,3584]{2,1,0:T(8,128)(2,1)} %all-gather.9.cloned.1.call-done, f32[512,256]{1,0:T(8,128)} %fusion.18), kind=kOutput, calls=%fused_computation.1 | convolution fusion | flops 1881669632 | bytes 11534336 | tf_op jit(solution)/shard_map/dot_general | solution.py:33
  103.7 35.4 %all-gather.5.cloned.1.call-done = bf16[64,8,3584]{2,1,0:T(8,128)(2,1)} async-done(((bf16[16,8,3584]{2,1,0:T(8,128)(2,1)}), bf16[64,8,3584]{2,1,0:T(8,128)(2,1)}) %all-gather.5.cloned.1.call-update) | async-done | bytes 3670032 | tf_op jit(solution)/shard_map/all_gather | solution.py:53
  139.2 4.5 fusion.26
  143.7 8.4 %convolution_convert_fusion.3 = bf16[512,3584]{1,0:T(8,128)(2,1)} fusion(bf16[1,1,256,3584]{3,2,1,0:T(8,128)(2,1)S(1)} %copy-done, bf16[1,1,3584,256]{3,2,1,0:T(8,128)(2,1)} %param.12, bf16[64,8,3584]{2,1,0:T(8,128)(2,1)} %all-gather.5.cloned.1.call-done, f32[512,256]{1,0:T(8,128)} %fusion.26), kind=kOutput, calls=%fused_computation.3 | convolution fusion | flops 1881669632 | bytes 11534336 | tf_op jit(solution)/shard_map/dot_general | solution.py:33
  152.2 35.1 %reduce-scatter.9.cloned.1.call-done = bf16[128,3584]{1,0:T(8,128)(2,1)} async-done(((bf16[512,3584]{1,0:T(8,128)(2,1)}), bf16[128,3584]{1,0:T(8,128)(2,1)}) %reduce-scatter.9.cloned.1.call-update) | async-done | bytes 917520 | tf_op jit(solution)/shard_map/reduce_scatter | solution.py:55
  187.3 7.8 %all-to-all-start.5 = ((bf16[16,8,3584]{2,1,0:T(8,128)(2,1)}), bf16[16,8,3584]{2,1,0:T(8,128)(2,1)}, u32[]{:S(2)}, u32[]{:S(2)}) async-start(bf16[16,8,3584]{2,1,0:T(8,128)(2,1)} %bitcast.186), calls=%async_computation.8 | async-start | bytes 1835008 | tf_op jit(solution)/shard_map/all_to_all | solution.py:56
  195.1 0.3 fusion.102
  195.4 25.1 %all-to-all-done.5 = bf16[16,8,3584]{2,1,0:T(8,128)(2,1)} async-done(((bf16[16,8,3584]{2,1,0:T(8,128)(2,1)}), bf16[16,8,3584]{2,1,0:T(8,128)(2,1)}, u32[]{:S(2)}, u32[]{:S(2)}) %all-to-all-start.5) | async-done | bytes 917536 | tf_op jit(solution)/shard_map/all_to_all | solution.py:56
  220.5 1.5 fusion.10
  222.0 1.3 collective-permute-start.2
  223.3 10.6 %collective-permute-done.2 = bf16[64,3584]{1,0:T(8,128)(2,1)S(1)} collective-permute-done((bf16[64,3584]{1,0:T(8,128)(2,1)S(1)}, bf16[64,3584]{1,0:T(8,128)(2,1)S(1)}, u32[]{:S(2)}, u32[]{:S(2)}) %collective-permute-start.2) | collective-permute-done | bytes 458784 | tf_op jit(solution)/shard_map/ppermute | solution.py:14
  234.1 0.5 fusion.7
  234.6 30.8 %all_to_all.42 = bf16[16,8,3584]{2,1,0:T(8,128)(2,1)} all-to-all(bf16[16,8,3584]{2,1,0:T(8,128)(2,1)S(1)} %fusion.7), channel_id=1, replica_groups=mesh['section'=4,'y'=4,'z'=8,'core'=2] {'z','core'}, dimensions={0} | all-to-all | bytes 1835008 | tf_op jit(solution)/shard_map/all_to_all | solution.py:52
  265.4 4.2 all-to-all-start.1
  269.9 0.3 fusion.100
  270.2 23.7 %all-to-all-done.1 = bf16[16,8,3584]{2,1,0:T(8,128)(2,1)} async-done(((bf16[16,8,3584]{2,1,0:T(8,128)(2,1)}), bf16[16,8,3584]{2,1,0:T(8,128)(2,1)}, u32[]{:S(2)}, u32[]{:S(2)}) %all-to-all-start.1) | async-done | bytes 917536 | tf_op jit(solution)/shard_map/all_to_all | solution.py:56
  293.9 1.5 fusion.8
  295.6 12.5 %collective-permute-done = bf16[64,3584]{1,0:T(8,128)(2,1)S(1)} collective-permute-done((bf16[64,3584]{1,0:T(8,128)(2,1)S(1)}, bf16[64,3584]{1,0:T(8,128)(2,1)S(1)}, u32[]{:S(2)}, u32[]{:S(2)}) %collective-permute-start) | collective-permute-done | bytes 458784 | tf_op jit(solution)/shard_map/ppermute | solution.py:14
  308.3 0.5 fusion.5
  308.7 30.4 %all_to_all.43 = bf16[16,8,3584]{2,1,0:T(8,128)(2,1)} all-to-all(bf16[16,8,3584]{2,1,0:T(8,128)(2,1)S(1)} %fusion.5), channel_id=1, replica_groups=mesh['section'=4,'y'=4,'z'=8,'core'=2] {'z','core'}, dimensions={0} | all-to-all | bytes 1835008 | tf_op jit(solution)/shard_map/all_to_all | solution.py:52
  339.2 4.5 fusion.14
  343.7 9.0 %convolution_convert_fusion = bf16[512,3584]{1,0:T(8,128)(2,1)} fusion(bf16[1,1,256,3584]{3,2,1,0:T(8,128)(2,1)S(1)} %copy-done, bf16[1,1,3584,256]{3,2,1,0:T(8,128)(2,1)} %param.12, bf16[64,8,3584]{2,1,0:T(8,128)(2,1)} %all-gather.11.cloned.1.call-done, f32[512,256]{1,0:T(8,128)} %fusion.14), kind=kOutput, calls=%fused_computation | convolution fusion | flops 1881669632 | bytes 11534336 | tf_op jit(solution)/shard_map/dot_general | solution.py:33
  352.8 25.4 %all-gather.7.cloned.1.call-done = bf16[64,8,3584]{2,1,0:T(8,128)(2,1)} async-done(((bf16[16,8,3584]{2,1,0:T(8,128)(2,1)}), bf16[64,8,3584]{2,1,0:T(8,128)(2,1)}) %all-gather.7.cloned.1.call-update) | async-done | bytes 3670032 | tf_op jit(solution)/shard_map/all_gather | solution.py:53
  378.1 4.5 fusion.22
  382.7 8.4 %convolution_convert_fusion.2 = bf16[512,3584]{1,0:T(8,128)(2,1)} fusion(bf16[1,1,256,3584]{3,2,1,0:T(8,128)(2,1)S(1)} %copy-done, bf16[1,1,3584,256]{3,2,1,0:T(8,128)(2,1)} %param.12, bf16[64,8,3584]{2,1,0:T(8,128)(2,1)} %all-gather.7.cloned.1.call-done, f32[512,256]{1,0:T(8,128)} %fusion.22), kind=kOutput, calls=%fused_computation.2 | convolution fusion | flops 1881669632 | bytes 11534336 | tf_op jit(solution)/shard_map/dot_general | solution.py:33
  391.1 35.1 %reduce-scatter.11.cloned.1.call-done = bf16[128,3584]{1,0:T(8,128)(2,1)} async-done(((bf16[512,3584]{1,0:T(8,128)(2,1)}), bf16[128,3584]{1,0:T(8,128)(2,1)}) %reduce-scatter.11.cloned.1.call-update) | async-done | bytes 917520 | tf_op jit(solution)/shard_map/reduce_scatter | solution.py:55
  426.2 7.8 %all-to-all-start.7 = ((bf16[16,8,3584]{2,1,0:T(8,128)(2,1)}), bf16[16,8,3584]{2,1,0:T(8,128)(2,1)}, u32[]{:S(2)}, u32[]{:S(2)}) async-start(bf16[16,8,3584]{2,1,0:T(8,128)(2,1)} %bitcast.187), calls=%async_computation.11 | async-start | bytes 1835008 | tf_op jit(solution)/shard_map/all_to_all | solution.py:56
  434.0 39.7 %reduce-scatter.7.cloned.1.call-done = bf16[128,3584]{1,0:T(8,128)(2,1)} async-done(((bf16[512,3584]{1,0:T(8,128)(2,1)}), bf16[128,3584]{1,0:T(8,128)(2,1)}) %reduce-scatter.7.cloned.1.call-update) | async-done | bytes 917520 | tf_op jit(solution)/shard_map/reduce_scatter | solution.py:55
  473.7 7.8 %all-to-all-start.3 = ((bf16[16,8,3584]{2,1,0:T(8,128)(2,1)}), bf16[16,8,3584]{2,1,0:T(8,128)(2,1)}, u32[]{:S(2)}, u32[]{:S(2)}) async-start(bf16[16,8,3584]{2,1,0:T(8,128)(2,1)} %bitcast.185), calls=%async_computation.5 | async-start | bytes 1835008 | tf_op jit(solution)/shard_map/all_to_all | solution.py:56
  481.5 0.3 fusion.103
  481.8 0.3 fusion.101
  482.1 2.3 fusion.11
  484.4 1.2 collective-permute-start.3
  485.6 21.3 %all-to-all-done.3 = bf16[16,8,3584]{2,1,0:T(8,128)(2,1)} async-done(((bf16[16,8,3584]{2,1,0:T(8,128)(2,1)}), bf16[16,8,3584]{2,1,0:T(8,128)(2,1)}, u32[]{:S(2)}, u32[]{:S(2)}) %all-to-all-start.3) | async-done | bytes 917536 | tf_op jit(solution)/shard_map/all_to_all | solution.py:56
  506.9 1.5 fusion.9
  508.5 1.3 collective-permute-start.1
  509.7 10.6 %collective-permute-done.1 = bf16[64,3584]{1,0:T(8,128)(2,1)S(1)} collective-permute-done((bf16[64,3584]{1,0:T(8,128)(2,1)S(1)}, bf16[64,3584]{1,0:T(8,128)(2,1)S(1)}, u32[]{:S(2)}, u32[]{:S(2)}) %collective-permute-start.1) | collective-permute-done | bytes 458784 | tf_op jit(solution)/shard_map/ppermute | solution.py:14
  520.3 1.0 maximum_bitcast_fusion
  (55 shorter events, 2.3 us)
Async XLA Ops:
  6.5 88.6 %copy-start = (bf16[1,1,256,3584]{3,2,1,0:T(8,128)(2,1)S(1)}, bf16[1,1,256,3584]{3,2,1,0:T(8,128)(2,1)}, u32[]{:S(2)}) copy-start(bf16[1,1,256,3584]{3,2,1,0:T(8,128)(2,1)} %param.13) | copy-start | bytes 5505028
  6.5 4.9 copy-start.1
  6.5 84.1 %all-gather.9.cloned.1.call-start = ((), (), s32[]{:S(2)}) async-start(), calls=%async_computation.16 | async-start | bytes 4587520 | tf_op jit(solution)/shard_map/all_gather | solution.py:53
  47.4 91.7 %all-gather.5.cloned.1.call-start = ((), (), s32[]{:S(2)}) async-start(), calls=%async_computation.12 | async-start | bytes 4587520 | tf_op jit(solution)/shard_map/all_gather | solution.py:53
  76.5 110.8 %reduce-scatter.9.cloned.1.call-start = ((), (), s32[]{:S(2)}) async-start(), calls=%async_computation.17 | async-start | bytes 4587520 | tf_op jit(solution)/shard_map/reduce_scatter | solution.py:55
  103.7 161.7 %reduce-scatter.5.cloned.1.call-start = ((), (), s32[]{:S(2)}) async-start(), calls=%async_computation.13 | async-start | bytes 4587520 | tf_op jit(solution)/shard_map/reduce_scatter | solution.py:55
  152.2 42.9 %copy-start.2 = (bf16[1,3584,16]{1,2,0:T(8,128)(2,1)S(1)}, bf16[1,3584,16]{1,2,0:T(8,128)(2,1)}, u32[]{:S(2)}) copy-start(bf16[1,3584,16]{1,2,0:T(8,128)(2,1)} %param.9) | copy-start | bytes 344068
  187.3 33.2 %all-to-all-start.5 = ((bf16[16,8,3584]{2,1,0:T(8,128)(2,1)}), bf16[16,8,3584]{2,1,0:T(8,128)(2,1)}, u32[]{:S(2)}, u32[]{:S(2)}) async-start(bf16[16,8,3584]{2,1,0:T(8,128)(2,1)} %bitcast.186), calls=%async_computation.8 | async-start | bytes 1835008 | tf_op jit(solution)/shard_map/all_to_all | solution.py:56
  195.0 144.2 %all-gather.11.cloned.1.call-start = ((), (), s32[]{:S(2)}) async-start(), calls=%async_computation.18 | async-start | bytes 4587520 | tf_op jit(solution)/shard_map/all_gather | solution.py:53
  222.0 11.9 %collective-permute-start.2 = (bf16[64,3584]{1,0:T(8,128)(2,1)S(1)}, bf16[64,3584]{1,0:T(8,128)(2,1)S(1)}, u32[]{:S(2)}, u32[]{:S(2)}) collective-permute-start(bf16[64,3584]{1,0:T(8,128)(2,1)S(1)} %fusion.10), channel_id=1, source_target_pairs={{0,64},{64,128},{128,192},{192,0},{1,65},{65,129},{129,193},{193,1... | collective-permute-start | bytes 1376264 | tf_op jit(solution)/shard_map/ppermute | solution.py:14
  265.4 28.5 %all-to-all-start.1 = ((bf16[16,8,3584]{2,1,0:T(8,128)(2,1)}), bf16[16,8,3584]{2,1,0:T(8,128)(2,1)}, u32[]{:S(2)}, u32[]{:S(2)}) async-start(bf16[16,8,3584]{2,1,0:T(8,128)(2,1)} %bitcast.184), calls=%async_computation.2 | async-start | bytes 1835008 | tf_op jit(solution)/shard_map/all_to_all | solution.py:56
  269.6 108.5 %all-gather.7.cloned.1.call-start = ((), (), s32[]{:S(2)}) async-start(), calls=%async_computation.14 | async-start | bytes 4587520 | tf_op jit(solution)/shard_map/all_gather | solution.py:53
  295.5 12.6 %collective-permute-start = (bf16[64,3584]{1,0:T(8,128)(2,1)S(1)}, bf16[64,3584]{1,0:T(8,128)(2,1)S(1)}, u32[]{:S(2)}, u32[]{:S(2)}) collective-permute-start(bf16[64,3584]{1,0:T(8,128)(2,1)S(1)} %fusion.8), channel_id=1, source_target_pairs={{0,64},{64,128},{128,192},{192,0},{1,65},{65,129},{129,193},{193,1... | collective-permute-start | bytes 1376264 | tf_op jit(solution)/shard_map/ppermute | solution.py:14
  339.1 87.1 %reduce-scatter.11.cloned.1.call-start = ((), (), s32[]{:S(2)}) async-start(), calls=%async_computation.19 | async-start | bytes 4587520 | tf_op jit(solution)/shard_map/reduce_scatter | solution.py:55
  352.7 121.0 %reduce-scatter.7.cloned.1.call-start = ((), (), s32[]{:S(2)}) async-start(), calls=%async_computation.15 | async-start | bytes 4587520 | tf_op jit(solution)/shard_map/reduce_scatter | solution.py:55
  426.2 47.5 %all-to-all-start.7 = ((bf16[16,8,3584]{2,1,0:T(8,128)(2,1)}), bf16[16,8,3584]{2,1,0:T(8,128)(2,1)}, u32[]{:S(2)}, u32[]{:S(2)}) async-start(bf16[16,8,3584]{2,1,0:T(8,128)(2,1)} %bitcast.187), calls=%async_computation.11 | async-start | bytes 1835008 | tf_op jit(solution)/shard_map/all_to_all | solution.py:56
  473.7 33.2 %all-to-all-start.3 = ((bf16[16,8,3584]{2,1,0:T(8,128)(2,1)}), bf16[16,8,3584]{2,1,0:T(8,128)(2,1)}, u32[]{:S(2)}, u32[]{:S(2)}) async-start(bf16[16,8,3584]{2,1,0:T(8,128)(2,1)} %bitcast.185), calls=%async_computation.5 | async-start | bytes 1835008 | tf_op jit(solution)/shard_map/all_to_all | solution.py:56
  484.4 25.3 %collective-permute-start.3 = (bf16[64,3584]{1,0:T(8,128)(2,1)}, bf16[64,3584]{1,0:T(8,128)(2,1)S(1)}, u32[]{:S(2)}, u32[]{:S(2)}) collective-permute-start(bf16[64,3584]{1,0:T(8,128)(2,1)} %fusion.11), channel_id=1, source_target_pairs={{0,64},{64,128},{128,192},{192,0},{1,65},{65,129},{129,193},{193,1... | collective-permute-start | bytes 1376264 | tf_op jit(solution)/shard_map/ppermute | solution.py:14
  508.5 11.9 %collective-permute-start.1 = (bf16[64,3584]{1,0:T(8,128)(2,1)S(1)}, bf16[64,3584]{1,0:T(8,128)(2,1)S(1)}, u32[]{:S(2)}, u32[]{:S(2)}) collective-permute-start(bf16[64,3584]{1,0:T(8,128)(2,1)S(1)} %fusion.9), channel_id=1, source_target_pairs={{0,64},{64,128},{128,192},{192,0},{1,65},{65,129},{129,193},{193,1... | collective-permute-start | bytes 1376264 | tf_op jit(solution)/shard_map/ppermute | solution.py:14
Sparse Core Ops, SparseCore 0:
  47.5 43.0 all-gather.8
  92.5 46.6 all-gather.4
  141.7 45.4 reduce-scatter.8
  189.7 44.8 reduce-scatter.4
  265.5 40.0 all-gather.10
  339.3 38.8 all-gather.6
  380.7 45.4 reduce-scatter.10
  428.8 44.8 reduce-scatter.6

commit v2 on v1

--- a/solution.py
+++ b/solution.py
@@ -50,9 +50,40 @@
         outbox = jnp.dot(placing, normed, preferred_element_type=jnp.float32).astype(jnp.bfloat16)
         outbox = outbox.reshape(row_size, capacity, width)
         arrived = lax.all_to_all(outbox, ROW, split_axis=0, concat_axis=0, tiled=True)
-        rows = lax.all_gather(arrived, "y", axis=0, tiled=True)
-        partial_out = expert_compute(rows.reshape(-1, width))
-        summed = lax.psum_scatter(partial_out, "y", scatter_dimension=0, tiled=True)
+        own = arrived.reshape(-1, width)
+        half = own.shape[0] // 2
+        from_below = passed_along(own, "y", 1)
+        from_above = passed_along(own, "y", -1)
+        far_low = passed_along(from_below[:half], "y", 1)
+        far_high = passed_along(from_above[half:], "y", -1)
+        rows = jnp.concatenate([own, from_below, from_above, far_low, far_high], axis=0)
+        partial_out = expert_compute(rows)
+        q_own, q_below, q_above, q_far_low, q_far_high = jnp.split(
+            partial_out, [own.shape[0], 2 * own.shape[0], 3 * own.shape[0], 3 * own.shape[0] + half]
+        )
+        back_below = passed_along(q_far_low, "y", -1)
+        back_above = passed_along(q_far_high, "y", 1)
+        direct_below = passed_along(q_below[half:], "y", -1)
+        direct_above = passed_along(q_above[:half], "y", 1)
+        relay_below = (q_below[:half].astype(jnp.float32) + back_below.astype(jnp.float32)).astype(
+            jnp.bfloat16
+        )
+        relay_above = (q_above[half:].astype(jnp.float32) + back_above.astype(jnp.float32)).astype(
+            jnp.bfloat16
+        )
+        late_below = passed_along(relay_below, "y", -1)
+        late_above = passed_along(relay_above, "y", 1)
+        lower = (
+            q_own[:half].astype(jnp.float32)
+            + direct_above.astype(jnp.float32)
+            + late_below.astype(jnp.float32)
+        )
+        upper = (
+            q_own[half:].astype(jnp.float32)
+            + direct_below.astype(jnp.float32)
+            + late_above.astype(jnp.float32)
+        )
+        summed = jnp.concatenate([lower, upper], axis=0).astype(jnp.bfloat16)
         back = lax.all_to_all(
             summed.reshape(row_size, capacity, width), ROW, split_axis=0, concat_axis=0, tiled=True
         )

time: 529 us -> 511 us (0.966); the launches traced: 528 us -> 502 us
  blocking collectives: 125 us -> 0 us
  starting transfers between devices: 31.8 us -> 101 us
  local copies, waits for them, and re-layouts: 1.31 us -> 42 us
  other arithmetic: 4.99 us -> 26.9 us
  waiting for transfers between devices: 289 us -> 276 us
  between operations: 13.7 us -> 0.74 us
  matrix products: 62.4 us -> 56 us
    all_to_all x4 -> x0, blocking collectives: 125 us -> none  [apply_layer(): lax.all_to_all(outbox, ROW, split_axis=0, concat_axis=0, tiled=True)]
    reduce_scatter x4 -> x0, waiting for transfers between devices: 110 us -> none  [apply_layer(): summed = lax.psum_scatter(partial_out, 'y', scatter_dimension=0, tiled=True)]
    ppermute x4 -> x44, waiting for transfers between devices: 33.7 us -> 142 us  [passed_along(): return lax.ppermute(value, axis, pairs)]
    all_gather x4 -> x0, waiting for transfers between devices: 74.9 us -> none  [apply_layer(): rows = lax.all_gather(arrived, 'y', axis=0, tiled=True)]
    all_to_all x0 -> x4, waiting for transfers between devices: none -> 73.9 us  [apply_layer(): lax.all_to_all(outbox, ROW, split_axis=0, concat_axis=0, tiled=True)]
    ppermute x4 -> x44, starting transfers between devices: 3.81 us -> 59.9 us  [passed_along(): return lax.ppermute(value, axis, pairs)]
    all_to_all x0 -> x4, starting transfers between devices: none -> 22.6 us  [apply_layer(): lax.all_to_all(outbox, ROW, split_axis=0, concat_axis=0, tiled=True)]
    unnamed x6 -> x52, local copies, waits for them, and re-layouts: 0.01 us -> 20.3 us
  transfers between devices with their start and end apart: 16 -> 52, of which waited for: 12 -> 24; matrix products, arithmetic and copies ran while one was open for 12% -> 22% of each run, Pallas kernels for 0% -> 0%
where the time goes in v2:
time: 511 us; the launch traced here: 502 us
  waiting for transfers between devices  276 us (54%)
  starting transfers between devices  101 us (20%)
  matrix products  56 us (11%)
  local copies, waits for them, and re-layouts  42 us (8%)
  other arithmetic  26.9 us (5%)
    ppermute x44, waiting for transfers between devices, passed_along(): return lax.ppermute(value, axis, pairs)  142 us
    all_to_all x4, waiting for transfers between devices, apply_layer(): lax.all_to_all(outbox, ROW, split_axis=0, concat_axis=0, tiled=True)  73.9 us
    ppermute x44, starting transfers between devices, passed_along(): return lax.ppermute(value, axis, pairs)  59.9 us
    all_to_all x4, waiting for transfers between devices, apply_layer(): lax.all_to_all(summed.reshape(row_size, capacity, width), ROW, split_axis...  59.4 us
    dot_general x4, matrix products, expert_compute(): jnp.dot(hidden, down_mat, preferred_element_type=jnp.float32)  33.6 us
    all_to_all x4, starting transfers between devices, apply_layer(): lax.all_to_all(outbox, ROW, split_axis=0, concat_axis=0, tiled=True)  22.6 us
    unnamed x52, local copies, waits for them, and re-layouts  20.3 us
    all_to_all x4, starting transfers between devices, apply_layer(): lax.all_to_all(summed.reshape(row_size, capacity, width), ROW, split_axis...  18.6 us
  transfers between devices with their start and end apart: 52, of which 24 were waited for; matrix products, arithmetic and copies ran while one was open for 22% of the time, Pallas kernels for 0%

profile of v2, /device:TPU:1, one launch (start us, length us, event | category | flops | bytes accessed | tf_op | source)
XLA Modules:
  0.0 502.4 jit_solution(3938127936456274108)
XLA Ops:
  4.9 2.4 fusion.4
  7.3 10.0 %all-to-all-start = ((bf16[16,8,3584]{2,1,0:T(8,128)(2,1)}), bf16[16,8,3584]{2,1,0:T(8,128)(2,1)}, u32[]{:S(2)}, u32[]{:S(2)}) async-start(bf16[16,8,3584]{2,1,0:T(8,128)(2,1)} %fusion.4), calls=%async_computation | async-start | bytes 1835008 | tf_op jit(solution)/shard_map/all_to_all | solution.py:52
  18.7 24.1 %all-to-all-done = bf16[16,8,3584]{2,1,0:T(8,128)(2,1)} async-done(((bf16[16,8,3584]{2,1,0:T(8,128)(2,1)}), bf16[16,8,3584]{2,1,0:T(8,128)(2,1)}, u32[]{:S(2)}, u32[]{:S(2)}) %all-to-all-start) | async-done | bytes 917536 | tf_op jit(solution)/shard_map/all_to_all | solution.py:52
  42.7 4.2 all-to-all-start.4
  49.9 21.5 %all-to-all-done.4 = bf16[16,8,3584]{2,1,0:T(8,128)(2,1)} async-done(((bf16[16,8,3584]{2,1,0:T(8,128)(2,1)}), bf16[16,8,3584]{2,1,0:T(8,128)(2,1)}, u32[]{:S(2)}, u32[]{:S(2)}) %all-to-all-start.4) | async-done | bytes 917536 | tf_op jit(solution)/shard_map/all_to_all | solution.py:52
  78.8 2.7 collective-permute-start.3
  81.6 13.7 %collective-permute-done.22 = bf16[128,3584]{1,0:T(8,128)(2,1)S(1)} collective-permute-done((bf16[128,3584]{1,0:T(8,128)(2,1)}, bf16[128,3584]{1,0:T(8,128)(2,1)S(1)}, u32[]{:S(2)}, u32[]{:S(2)}) %collective-permute-start.22) | collective-permute-done | bytes 917536 | tf_op jit(solution)/shard_map/ppermute | solution.py:14
  96.9 3.2 collective-permute-start.25
  109.1 8.4 %convolution_convert_fusion.3 = bf16[512,3584]{1,0:T(8,128)(2,1)} fusion(bf16[1,1,256,3584]{3,2,1,0:T(8,128)(2,1)S(1)} %copy-done, f32[512,256]{1,0:T(8,128)} %fusion.22, bf16[512,3584]{1,0:T(8,128)(2,1)} %copy-done.11, bf16[1,1,3584,256]{3,2,1,0:T(8,128)(2,1)} %param.11), kind=kOutput, calls=%fused_computation.3 | convolution fusion | flops 1881669632 | bytes 11534336 | tf_op jit(solution)/shard_map/dot_general | solution.py:33
  117.5 2.8 fusion.123
  120.4 2.6 collective-permute-start.5
  123.1 2.6 collective-permute-start.7
  131.6 8.4 %convolution_convert_fusion.1 = bf16[512,3584]{1,0:T(8,128)(2,1)} fusion(bf16[1,1,256,3584]{3,2,1,0:T(8,128)(2,1)S(1)} %copy-done, f32[512,256]{1,0:T(8,128)} %fusion.18, bf16[512,3584]{1,0:T(8,128)(2,1)} %copy-done.7, bf16[1,1,3584,256]{3,2,1,0:T(8,128)(2,1)} %param.11), kind=kOutput, calls=%fused_computation.1 | convolution fusion | flops 1881669632 | bytes 11534336 | tf_op jit(solution)/shard_map/dot_general | solution.py:33
  140.1 2.5 fusion.125
  145.3 8.8 %collective-permute-done.27 = bf16[64,3584]{1,0:T(8,128)(2,1)S(1)} collective-permute-done((bf16[64,3584]{1,0:T(8,128)(2,1)S(1)}, bf16[64,3584]{1,0:T(8,128)(2,1)S(1)}, u32[]{:S(2)}, u32[]{:S(2)}) %collective-permute-start.27) | collective-permute-done | bytes 458784 | tf_op jit(solution)/shard_map/ppermute | solution.py:14
  154.1 2.6 collective-permute-start.6
  157.9 2.7 collective-permute-start.29
  160.6 6.1 %collective-permute-done.6 = bf16[64,3584]{1,0:T(8,128)(2,1)S(1)} collective-permute-done((bf16[64,3584]{1,0:T(8,128)(2,1)S(1)}, bf16[64,3584]{1,0:T(8,128)(2,1)S(1)}, u32[]{:S(2)}, u32[]{:S(2)}) %collective-permute-start.6) | collective-permute-done | bytes 458784 | tf_op jit(solution)/shard_map/ppermute | solution.py:14
  166.7 3.3 collective-permute-start.28
  171.4 14.8 %collective-permute-done.28 = bf16[64,3584]{1,0:T(8,128)(2,1)S(1)} collective-permute-done((bf16[64,3584]{1,0:T(8,128)(2,1)S(1)}, bf16[64,3584]{1,0:T(8,128)(2,1)S(1)}, u32[]{:S(2)}, u32[]{:S(2)}) %collective-permute-start.28) | collective-permute-done | bytes 458784 | tf_op jit(solution)/shard_map/ppermute | solution.py:14
  190.7 5.0 all-to-all-start.1
  195.7 6.6 %collective-permute-done.31 = bf16[64,3584]{1,0:T(8,128)(2,1)} collective-permute-done((bf16[64,3584]{1,0:T(8,128)(2,1)}, bf16[64,3584]{1,0:T(8,128)(2,1)}, u32[]{:S(2)}, u32[]{:S(2)}) %collective-permute-start.31) | collective-permute-done | bytes 458784 | tf_op jit(solution)/shard_map/ppermute | solution.py:14
  204.8 16.4 %all-to-all-done.1 = bf16[16,8,3584]{2,1,0:T(8,128)(2,1)} async-done(((bf16[16,8,3584]{2,1,0:T(8,128)(2,1)}), bf16[16,8,3584]{2,1,0:T(8,128)(2,1)}, u32[]{:S(2)}, u32[]{:S(2)}) %all-to-all-start.1) | async-done | bytes 917536 | tf_op jit(solution)/shard_map/all_to_all | solution.py:87
  221.2 4.2 all-to-all-start.5
  228.5 12.3 %collective-permute-done.10 = bf16[64,3584]{1,0:T(8,128)(2,1)S(1)} collective-permute-done((bf16[64,3584]{1,0:T(8,128)(2,1)S(1)}, bf16[64,3584]{1,0:T(8,128)(2,1)S(1)}, u32[]{:S(2)}, u32[]{:S(2)}) %collective-permute-start.10) | collective-permute-done | bytes 458784 | tf_op jit(solution)/shard_map/ppermute | solution.py:14
  242.5 7.4 %all-to-all-done.5 = bf16[16,8,3584]{2,1,0:T(8,128)(2,1)} async-done(((bf16[16,8,3584]{2,1,0:T(8,128)(2,1)}), bf16[16,8,3584]{2,1,0:T(8,128)(2,1)}, u32[]{:S(2)}, u32[]{:S(2)}) %all-to-all-start.5) | async-done | bytes 917536 | tf_op jit(solution)/shard_map/all_to_all | solution.py:87
  249.8 4.2 all-to-all-start.2
  257.2 12.4 %collective-permute-done.32 = bf16[64,3584]{1,0:T(8,128)(2,1)S(1)} collective-permute-done((bf16[64,3584]{1,0:T(8,128)(2,1)S(1)}, bf16[64,3584]{1,0:T(8,128)(2,1)S(1)}, u32[]{:S(2)}, u32[]{:S(2)}) %collective-permute-start.32) | collective-permute-done | bytes 458784 | tf_op jit(solution)/shard_map/ppermute | solution.py:14
  271.2 7.4 %all-to-all-done.2 = bf16[16,8,3584]{2,1,0:T(8,128)(2,1)} async-done(((bf16[16,8,3584]{2,1,0:T(8,128)(2,1)}), bf16[16,8,3584]{2,1,0:T(8,128)(2,1)}, u32[]{:S(2)}, u32[]{:S(2)}) %all-to-all-start.2) | async-done | bytes 917536 | tf_op jit(solution)/shard_map/all_to_all | solution.py:52
  278.6 4.2 all-to-all-start.6
  286.4 20.9 %all-to-all-done.6 = bf16[16,8,3584]{2,1,0:T(8,128)(2,1)} async-done(((bf16[16,8,3584]{2,1,0:T(8,128)(2,1)}), bf16[16,8,3584]{2,1,0:T(8,128)(2,1)}, u32[]{:S(2)}, u32[]{:S(2)}) %all-to-all-start.6) | async-done | bytes 917536 | tf_op jit(solution)/shard_map/all_to_all | solution.py:52
  318.4 13.6 %collective-permute-done.33 = bf16[128,3584]{1,0:T(8,128)(2,1)S(1)} collective-permute-done((bf16[128,3584]{1,0:T(8,128)(2,1)}, bf16[128,3584]{1,0:T(8,128)(2,1)S(1)}, u32[]{:S(2)}, u32[]{:S(2)}) %collective-permute-start.33) | collective-permute-done | bytes 917536 | tf_op jit(solution)/shard_map/ppermute | solution.py:14
  339.1 2.8 collective-permute-done.13
  347.0 8.4 %convolution_convert_fusion.2 = bf16[512,3584]{1,0:T(8,128)(2,1)} fusion(bf16[1,1,256,3584]{3,2,1,0:T(8,128)(2,1)S(1)} %copy-done, f32[512,256]{1,0:T(8,128)} %fusion.20, bf16[512,3584]{1,0:T(8,128)(2,1)} %copy-done.12, bf16[1,1,3584,256]{3,2,1,0:T(8,128)(2,1)} %param.11), kind=kOutput, calls=%fused_computation.2 | convolution fusion | flops 1881669632 | bytes 11534336 | tf_op jit(solution)/shard_map/dot_general | solution.py:33
  355.4 2.8 fusion.122
  368.9 8.4 %convolution_convert_fusion = bf16[512,3584]{1,0:T(8,128)(2,1)} fusion(bf16[1,1,256,3584]{3,2,1,0:T(8,128)(2,1)S(1)} %copy-done, f32[512,256]{1,0:T(8,128)} %fusion.16, bf16[512,3584]{1,0:T(8,128)(2,1)} %copy-done.10, bf16[1,1,3584,256]{3,2,1,0:T(8,128)(2,1)} %param.11), kind=kOutput, calls=%fused_computation | convolution fusion | flops 1881669632 | bytes 11534336 | tf_op jit(solution)/shard_map/dot_general | solution.py:33
  377.3 2.5 fusion.124
  382.4 8.9 %collective-permute-done.38 = bf16[64,3584]{1,0:T(8,128)(2,1)S(1)} collective-permute-done((bf16[64,3584]{1,0:T(8,128)(2,1)S(1)}, bf16[64,3584]{1,0:T(8,128)(2,1)S(1)}, u32[]{:S(2)}, u32[]{:S(2)}) %collective-permute-start.38) | collective-permute-done | bytes 458784 | tf_op jit(solution)/shard_map/ppermute | solution.py:14
  394.8 2.7 collective-permute-start.40
  397.5 6.5 %collective-permute-done.17 = bf16[64,3584]{1,0:T(8,128)(2,1)S(1)} collective-permute-done((bf16[64,3584]{1,0:T(8,128)(2,1)S(1)}, bf16[64,3584]{1,0:T(8,128)(2,1)S(1)}, u32[]{:S(2)}, u32[]{:S(2)}) %collective-permute-start.17) | collective-permute-done | bytes 458784 | tf_op jit(solution)/shard_map/ppermute | solution.py:14
  403.9 3.3 collective-permute-start.39
  408.8 14.7 %collective-permute-done.39 = bf16[64,3584]{1,0:T(8,128)(2,1)S(1)} collective-permute-done((bf16[64,3584]{1,0:T(8,128)(2,1)S(1)}, bf16[64,3584]{1,0:T(8,128)(2,1)S(1)}, u32[]{:S(2)}, u32[]{:S(2)}) %collective-permute-start.39) | collective-permute-done | bytes 458784 | tf_op jit(solution)/shard_map/ppermute | solution.py:14
  428.3 5.0 %all-to-all-start.3 = ((bf16[16,8,3584]{2,1,0:T(8,128)(2,1)}), bf16[16,8,3584]{2,1,0:T(8,128)(2,1)}, u32[]{:S(2)}, u32[]{:S(2)}) async-start(bf16[16,8,3584]{2,1,0:T(8,128)(2,1)} %maximum_bitcast_fusion.1), calls=%async_computation.3 | async-start | bytes 1835008 | tf_op jit(solution)/shard_map/all_to_all | solution.py:87
  433.3 6.7 %collective-permute-done.42 = bf16[64,3584]{1,0:T(8,128)(2,1)} collective-permute-done((bf16[64,3584]{1,0:T(8,128)(2,1)}, bf16[64,3584]{1,0:T(8,128)(2,1)}, u32[]{:S(2)}, u32[]{:S(2)}) %collective-permute-start.42) | collective-permute-done | bytes 458784 | tf_op jit(solution)/shard_map/ppermute | solution.py:14
  443.5 15.3 %all-to-all-done.3 = bf16[16,8,3584]{2,1,0:T(8,128)(2,1)} async-done(((bf16[16,8,3584]{2,1,0:T(8,128)(2,1)}), bf16[16,8,3584]{2,1,0:T(8,128)(2,1)}, u32[]{:S(2)}, u32[]{:S(2)}) %all-to-all-start.3) | async-done | bytes 917536 | tf_op jit(solution)/shard_map/all_to_all | solution.py:87
  458.9 4.4 all-to-all-start.7
  467.4 20.3 %all-to-all-done.7 = bf16[16,8,3584]{2,1,0:T(8,128)(2,1)} async-done(((bf16[16,8,3584]{2,1,0:T(8,128)(2,1)}), bf16[16,8,3584]{2,1,0:T(8,128)(2,1)}, u32[]{:S(2)}, u32[]{:S(2)}) %all-to-all-start.7) | async-done | bytes 917536 | tf_op jit(solution)/shard_map/all_to_all | solution.py:87
  490.5 10.7 %collective-permute-done.43 = bf16[64,3584]{1,0:T(8,128)(2,1)S(1)} collective-permute-done((bf16[64,3584]{1,0:T(8,128)(2,1)S(1)}, bf16[64,3584]{1,0:T(8,128)(2,1)S(1)}, u32[]{:S(2)}, u32[]{:S(2)}) %collective-permute-start.43) | collective-permute-done | bytes 458784 | tf_op jit(solution)/shard_map/ppermute | solution.py:14
  (193 shorter events, 116.1 us)
Async XLA Ops:
  7.3 35.4 %all-to-all-start = ((bf16[16,8,3584]{2,1,0:T(8,128)(2,1)}), bf16[16,8,3584]{2,1,0:T(8,128)(2,1)}, u32[]{:S(2)}, u32[]{:S(2)}) async-start(bf16[16,8,3584]{2,1,0:T(8,128)(2,1)} %fusion.4), calls=%async_computation | async-start | bytes 1835008 | tf_op jit(solution)/shard_map/all_to_all | solution.py:52
  42.7 28.7 %all-to-all-start.4 = ((bf16[16,8,3584]{2,1,0:T(8,128)(2,1)}), bf16[16,8,3584]{2,1,0:T(8,128)(2,1)}, u32[]{:S(2)}, u32[]{:S(2)}) async-start(bf16[16,8,3584]{2,1,0:T(8,128)(2,1)} %fusion.6), calls=%async_computation.4 | async-start | bytes 1835008 | tf_op jit(solution)/shard_map/all_to_all | solution.py:52
  47.0 29.7 %collective-permute-start = (bf16[128,3584]{1,0:T(8,128)(2,1)}, bf16[128,3584]{1,0:T(8,128)(2,1)}, u32[]{:S(2)}, u32[]{:S(2)}) collective-permute-start(bf16[128,3584]{1,0:T(8,128)(2,1)} %bitcast.5), channel_id=1, source_target_pairs={{0,16},{16,32},{32,48},{48,0},{1,17},{17,33},{33,49},{49,1},{2,18}... | collective-permute-start | bytes 2752520 | tf_op jit(solution)/shard_map/ppermute | solution.py:14
  48.3 29.5 %collective-permute-start.1 = (bf16[128,3584]{1,0:T(8,128)(2,1)}, bf16[128,3584]{1,0:T(8,128)(2,1)}, u32[]{:S(2)}, u32[]{:S(2)}) collective-permute-start(bf16[128,3584]{1,0:T(8,128)(2,1)} %bitcast.5), channel_id=1, source_target_pairs={{0,48},{16,0},{32,16},{48,32},{1,49},{17,1},{33,17},{49,33},{2,50}... | collective-permute-start | bytes 2752520 | tf_op jit(solution)/shard_map/ppermute | solution.py:14
  71.4 23.8 %collective-permute-start.22 = (bf16[128,3584]{1,0:T(8,128)(2,1)}, bf16[128,3584]{1,0:T(8,128)(2,1)S(1)}, u32[]{:S(2)}, u32[]{:S(2)}) collective-permute-start(bf16[128,3584]{1,0:T(8,128)(2,1)} %bitcast.21), channel_id=1, source_target_pairs={{0,16},{16,32},{32,48},{48,0},{1,17},{17,33},{33,49},{49,1},{2,18}... | collective-permute-start | bytes 2752520 | tf_op jit(solution)/shard_map/ppermute | solution.py:14
  72.7 23.4 %collective-permute-start.23 = (bf16[128,3584]{1,0:T(8,128)(2,1)}, bf16[128,3584]{1,0:T(8,128)(2,1)S(1)}, u32[]{:S(2)}, u32[]{:S(2)}) collective-permute-start(bf16[128,3584]{1,0:T(8,128)(2,1)} %bitcast.21), channel_id=1, source_target_pairs={{0,48},{16,0},{32,16},{48,32},{1,49},{17,1},{33,17},{49,33},{2,50}... | collective-permute-start | bytes 2752520 | tf_op jit(solution)/shard_map/ppermute | solution.py:14
  77.7 27.5 %collective-permute-start.2 = (bf16[64,3584]{1,0:T(8,128)(2,1)S(1)}, bf16[64,3584]{1,0:T(8,128)(2,1)S(1)}, u32[]{:S(2)}, u32[]{:S(2)}) collective-permute-start(bf16[64,3584]{1,0:T(8,128)(2,1)S(1)} %slice.176), channel_id=1, source_target_pairs={{0,16},{16,32},{32,48},{48,0},{1,17},{17,33},{33,49},{49,1},{2,18}... | collective-permute-start | bytes 1376264 | tf_op jit(solution)/shard_map/ppermute | solution.py:14
  78.8 26.4 %collective-permute-start.3 = (bf16[64,3584]{1,0:T(8,128)(2,1)S(1)}, bf16[64,3584]{1,0:T(8,128)(2,1)S(1)}, u32[]{:S(2)}, u32[]{:S(2)}) collective-permute-start(bf16[64,3584]{1,0:T(8,128)(2,1)S(1)} %slice.177), channel_id=1, source_target_pairs={{0,48},{16,0},{32,16},{48,32},{1,49},{17,1},{33,17},{49,33},{2,50}... | collective-permute-start | bytes 1376264 | tf_op jit(solution)/shard_map/ppermute | solution.py:14
  96.1 27.0 %collective-permute-start.24 = (bf16[64,3584]{1,0:T(8,128)(2,1)}, bf16[64,3584]{1,0:T(8,128)(2,1)}, u32[]{:S(2)}, u32[]{:S(2)}) collective-permute-start(bf16[64,3584]{1,0:T(8,128)(2,1)} %slice.192), channel_id=1, source_target_pairs={{0,16},{16,32},{32,48},{48,0},{1,17},{17,33},{33,49},{49,1},{2,18}... | collective-permute-start | bytes 1376264 | tf_op jit(solution)/shard_map/ppermute | solution.py:14
  96.9 29.8 %collective-permute-start.25 = (bf16[64,3584]{1,0:T(8,128)(2,1)}, bf16[64,3584]{1,0:T(8,128)(2,1)}, u32[]{:S(2)}, u32[]{:S(2)}) collective-permute-start(bf16[64,3584]{1,0:T(8,128)(2,1)} %slice.193), channel_id=1, source_target_pairs={{0,48},{16,0},{32,16},{48,32},{1,49},{17,1},{33,17},{49,33},{2,50}... | collective-permute-start | bytes 1376264 | tf_op jit(solution)/shard_map/ppermute | solution.py:14
  120.4 23.6 %collective-permute-start.5 = (bf16[64,3584]{1,0:T(8,128)(2,1)}, bf16[64,3584]{1,0:T(8,128)(2,1)}, u32[]{:S(2)}, u32[]{:S(2)}) collective-permute-start(bf16[64,3584]{1,0:T(8,128)(2,1)} %get-tuple-element.18), channel_id=1, source_target_pairs={{0,48},{16,0},{32,16},{48,32},{1,49},{17,1},{33,17},{49,33},{2,50}... | collective-permute-start | bytes 1376264 | tf_op jit(solution)/shard_map/ppermute | solution.py:14
  123.0 34.8 %collective-permute-start.4 = (bf16[64,3584]{1,0:T(8,128)(2,1)}, bf16[64,3584]{1,0:T(8,128)(2,1)S(1)}, u32[]{:S(2)}, u32[]{:S(2)}) collective-permute-start(bf16[64,3584]{1,0:T(8,128)(2,1)} %get-tuple-element.15), channel_id=1, source_target_pairs={{0,16},{16,32},{32,48},{48,0},{1,17},{17,33},{33,49},{49,1},{2,18}... | collective-permute-start | bytes 1376264 | tf_op jit(solution)/shard_map/ppermute | solution.py:14
  123.0 34.9 %collective-permute-start.8 = (bf16[64,3584]{1,0:T(8,128)(2,1)}, bf16[64,3584]{1,0:T(8,128)(2,1)}, u32[]{:S(2)}, u32[]{:S(2)}) collective-permute-start(bf16[64,3584]{1,0:T(8,128)(2,1)} %get-tuple-element.16), channel_id=1, source_target_pairs={{0,16},{16,32},{32,48},{48,0},{1,17},{17,33},{33,49},{49,1},{2,18}... | collective-permute-start | bytes 1376264 | tf_op jit(solution)/shard_map/ppermute | solution.py:14
  123.1 65.4 %collective-permute-start.7 = (bf16[64,3584]{1,0:T(8,128)(2,1)}, bf16[64,3584]{1,0:T(8,128)(2,1)}, u32[]{:S(2)}, u32[]{:S(2)}) collective-permute-start(bf16[64,3584]{1,0:T(8,128)(2,1)} %get-tuple-element.17), channel_id=1, source_target_pairs={{0,48},{16,0},{32,16},{48,32},{1,49},{17,1},{33,17},{49,33},{2,50}... | collective-permute-start | bytes 1376264 | tf_op jit(solution)/shard_map/ppermute | solution.py:14
  144.0 27.3 %collective-permute-start.26 = (bf16[64,3584]{1,0:T(8,128)(2,1)S(1)}, bf16[64,3584]{1,0:T(8,128)(2,1)S(1)}, u32[]{:S(2)}, u32[]{:S(2)}) collective-permute-start(bf16[64,3584]{1,0:T(8,128)(2,1)S(1)} %get-tuple-element.27), channel_id=1, source_target_pairs={{0,16},{16,32},{32,48},{48,0},{1,17},{17,33},{33,49},{49,1},{2,18}... | collective-permute-start | bytes 1376264 | tf_op jit(solution)/shard_map/ppermute | solution.py:14
  154.1 12.6 %collective-permute-start.6 = (bf16[64,3584]{1,0:T(8,128)(2,1)S(1)}, bf16[64,3584]{1,0:T(8,128)(2,1)S(1)}, u32[]{:S(2)}, u32[]{:S(2)}) collective-permute-start(bf16[64,3584]{1,0:T(8,128)(2,1)S(1)} %add_convert_fusion.15), channel_id=1, source_target_pairs={{0,48},{16,0},{32,16},{48,32},{1,49},{17,1},{33,17},{49,33},{2,50}... | collective-permute-start | bytes 1376264 | tf_op jit(solution)/shard_map/ppermute | solution.py:14
  157.8 13.6 %collective-permute-start.30 = (bf16[64,3584]{1,0:T(8,128)(2,1)S(1)}, bf16[64,3584]{1,0:T(8,128)(2,1)S(1)}, u32[]{:S(2)}, u32[]{:S(2)}) collective-permute-start(bf16[64,3584]{1,0:T(8,128)(2,1)S(1)} %get-tuple-element.28), channel_id=1, source_target_pairs={{0,16},{16,32},{32,48},{48,0},{1,17},{17,33},{33,49},{49,1},{2,18}... | collective-permute-start | bytes 1376264 | tf_op jit(solution)/shard_map/ppermute | solution.py:14
  157.9 37.7 %collective-permute-start.29 = (bf16[64,3584]{1,0:T(8,128)(2,1)}, bf16[64,3584]{1,0:T(8,128)(2,1)}, u32[]{:S(2)}, u32[]{:S(2)}) collective-permute-start(bf16[64,3584]{1,0:T(8,128)(2,1)} %get-tuple-element.29), channel_id=1, source_target_pairs={{0,48},{16,0},{32,16},{48,32},{1,49},{17,1},{33,17},{49,33},{2,50}... | collective-permute-start | bytes 1376264 | tf_op jit(solution)/shard_map/ppermute | solution.py:14
  166.7 19.6 %collective-permute-start.28 = (bf16[64,3584]{1,0:T(8,128)(2,1)S(1)}, bf16[64,3584]{1,0:T(8,128)(2,1)S(1)}, u32[]{:S(2)}, u32[]{:S(2)}) collective-permute-start(bf16[64,3584]{1,0:T(8,128)(2,1)S(1)} %add_convert_fusion.7), channel_id=1, source_target_pairs={{0,48},{16,0},{32,16},{48,32},{1,49},{17,1},{33,17},{49,33},{2,50}... | collective-permute-start | bytes 1376264 | tf_op jit(solution)/shard_map/ppermute | solution.py:14
  171.3 17.2 %collective-permute-start.9 = (bf16[64,3584]{1,0:T(8,128)(2,1)S(1)}, bf16[64,3584]{1,0:T(8,128)(2,1)S(1)}, u32[]{:S(2)}, u32[]{:S(2)}) collective-permute-start(bf16[64,3584]{1,0:T(8,128)(2,1)S(1)} %get-tuple-element.14), channel_id=1, source_target_pairs={{0,16},{16,32},{32,48},{48,0},{1,17},{17,33},{33,49},{49,1},{2,18}... | collective-permute-start | bytes 1376264 | tf_op jit(solution)/shard_map/ppermute | solution.py:14
  188.5 13.8 %collective-permute-start.31 = (bf16[64,3584]{1,0:T(8,128)(2,1)}, bf16[64,3584]{1,0:T(8,128)(2,1)}, u32[]{:S(2)}, u32[]{:S(2)}) collective-permute-start(bf16[64,3584]{1,0:T(8,128)(2,1)} %get-tuple-element.26), channel_id=1, source_target_pairs={{0,16},{16,32},{32,48},{48,0},{1,17},{17,33},{33,49},{49,1},{2,18}... | collective-permute-start | bytes 1376264 | tf_op jit(solution)/shard_map/ppermute | solution.py:14
  190.7 30.5 %all-to-all-start.1 = ((bf16[16,8,3584]{2,1,0:T(8,128)(2,1)}), bf16[16,8,3584]{2,1,0:T(8,128)(2,1)}, u32[]{:S(2)}, u32[]{:S(2)}) async-start(bf16[16,8,3584]{2,1,0:T(8,128)(2,1)} %maximum_bitcast_fusion), calls=%async_computation.1 | async-start | bytes 1835008 | tf_op jit(solution)/shard_map/all_to_all | solution.py:87
  221.2 28.7 %all-to-all-start.5 = ((bf16[16,8,3584]{2,1,0:T(8,128)(2,1)}), bf16[16,8,3584]{2,1,0:T(8,128)(2,1)}, u32[]{:S(2)}, u32[]{:S(2)}) async-start(bf16[16,8,3584]{2,1,0:T(8,128)(2,1)} %maximum_bitcast_fusion.2), calls=%async_computation.5 | async-start | bytes 1835008 | tf_op jit(solution)/shard_map/all_to_all | solution.py:87
  227.3 13.6 %collective-permute-start.10 = (bf16[64,3584]{1,0:T(8,128)(2,1)S(1)}, bf16[64,3584]{1,0:T(8,128)(2,1)S(1)}, u32[]{:S(2)}, u32[]{:S(2)}) collective-permute-start(bf16[64,3584]{1,0:T(8,128)(2,1)S(1)} %fusion.8), channel_id=1, source_target_pairs={{0,64},{64,128},{128,192},{192,0},{1,65},{65,129},{129,193},{193,1... | collective-permute-start | bytes 1376264 | tf_op jit(solution)/shard_map/ppermute | solution.py:14
  249.8 28.7 %all-to-all-start.2 = ((bf16[16,8,3584]{2,1,0:T(8,128)(2,1)}), bf16[16,8,3584]{2,1,0:T(8,128)(2,1)}, u32[]{:S(2)}, u32[]{:S(2)}) async-start(bf16[16,8,3584]{2,1,0:T(8,128)(2,1)} %fusion.5), calls=%async_computation.2 | async-start | bytes 1835008 | tf_op jit(solution)/shard_map/all_to_all | solution.py:52
  255.9 13.7 %collective-permute-start.32 = (bf16[64,3584]{1,0:T(8,128)(2,1)S(1)}, bf16[64,3584]{1,0:T(8,128)(2,1)S(1)}, u32[]{:S(2)}, u32[]{:S(2)}) collective-permute-start(bf16[64,3584]{1,0:T(8,128)(2,1)S(1)} %fusion.10), channel_id=1, source_target_pairs={{0,64},{64,128},{128,192},{192,0},{1,65},{65,129},{129,193},{193,1... | collective-permute-start | bytes 1376264 | tf_op jit(solution)/shard_map/ppermute | solution.py:14
  278.6 28.7 %all-to-all-start.6 = ((bf16[16,8,3584]{2,1,0:T(8,128)(2,1)}), bf16[16,8,3584]{2,1,0:T(8,128)(2,1)}, u32[]{:S(2)}, u32[]{:S(2)}) async-start(bf16[16,8,3584]{2,1,0:T(8,128)(2,1)} %fusion.7), calls=%async_computation.6 | async-start | bytes 1835008 | tf_op jit(solution)/shard_map/all_to_all | solution.py:52
  282.8 30.7 %collective-permute-start.11 = (bf16[128,3584]{1,0:T(8,128)(2,1)}, bf16[128,3584]{1,0:T(8,128)(2,1)}, u32[]{:S(2)}, u32[]{:S(2)}) collective-permute-start(bf16[128,3584]{1,0:T(8,128)(2,1)} %bitcast.13), channel_id=1, source_target_pairs={{0,16},{16,32},{32,48},{48,0},{1,17},{17,33},{33,49},{49,1},{2,18}... | collective-permute-start | bytes 2752520 | tf_op jit(solution)/shard_map/ppermute | solution.py:14
  284.7 30.9 %collective-permute-start.12 = (bf16[128,3584]{1,0:T(8,128)(2,1)}, bf16[128,3584]{1,0:T(8,128)(2,1)}, u32[]{:S(2)}, u32[]{:S(2)}) collective-permute-start(bf16[128,3584]{1,0:T(8,128)(2,1)} %bitcast.13), channel_id=1, source_target_pairs={{0,48},{16,0},{32,16},{48,32},{1,49},{17,1},{33,17},{49,33},{2,50}... | collective-permute-start | bytes 2752520 | tf_op jit(solution)/shard_map/ppermute | solution.py:14
  307.3 24.7 %collective-permute-start.33 = (bf16[128,3584]{1,0:T(8,128)(2,1)}, bf16[128,3584]{1,0:T(8,128)(2,1)S(1)}, u32[]{:S(2)}, u32[]{:S(2)}) collective-permute-start(bf16[128,3584]{1,0:T(8,128)(2,1)} %bitcast.26), channel_id=1, source_target_pairs={{0,16},{16,32},{32,48},{48,0},{1,17},{17,33},{33,49},{49,1},{2,18}... | collective-permute-start | bytes 2752520 | tf_op jit(solution)/shard_map/ppermute | solution.py:14
  309.4 24.0 %collective-permute-start.34 = (bf16[128,3584]{1,0:T(8,128)(2,1)}, bf16[128,3584]{1,0:T(8,128)(2,1)S(1)}, u32[]{:S(2)}, u32[]{:S(2)}) collective-permute-start(bf16[128,3584]{1,0:T(8,128)(2,1)} %bitcast.26), channel_id=1, source_target_pairs={{0,48},{16,0},{32,16},{48,32},{1,49},{17,1},{33,17},{49,33},{2,50}... | collective-permute-start | bytes 2752520 | tf_op jit(solution)/shard_map/ppermute | solution.py:14
  314.5 27.4 %collective-permute-start.13 = (bf16[64,3584]{1,0:T(8,128)(2,1)S(1)}, bf16[64,3584]{1,0:T(8,128)(2,1)S(1)}, u32[]{:S(2)}, u32[]{:S(2)}) collective-permute-start(bf16[64,3584]{1,0:T(8,128)(2,1)S(1)} %slice.184), channel_id=1, source_target_pairs={{0,16},{16,32},{32,48},{48,0},{1,17},{17,33},{33,49},{49,1},{2,18}... | collective-permute-start | bytes 1376264 | tf_op jit(solution)/shard_map/ppermute | solution.py:14
  316.7 26.4 %collective-permute-start.14 = (bf16[64,3584]{1,0:T(8,128)(2,1)S(1)}, bf16[64,3584]{1,0:T(8,128)(2,1)S(1)}, u32[]{:S(2)}, u32[]{:S(2)}) collective-permute-start(bf16[64,3584]{1,0:T(8,128)(2,1)S(1)} %slice.185), channel_id=1, source_target_pairs={{0,48},{16,0},{32,16},{48,32},{1,49},{17,1},{33,17},{49,33},{2,50}... | collective-permute-start | bytes 1376264 | tf_op jit(solution)/shard_map/ppermute | solution.py:14
  332.8 28.3 %collective-permute-start.35 = (bf16[64,3584]{1,0:T(8,128)(2,1)}, bf16[64,3584]{1,0:T(8,128)(2,1)}, u32[]{:S(2)}, u32[]{:S(2)}) collective-permute-start(bf16[64,3584]{1,0:T(8,128)(2,1)} %slice.200), channel_id=1, source_target_pairs={{0,16},{16,32},{32,48},{48,0},{1,17},{17,33},{33,49},{49,1},{2,18}... | collective-permute-start | bytes 1376264 | tf_op jit(solution)/shard_map/ppermute | solution.py:14
  334.2 29.8 %collective-permute-start.36 = (bf16[64,3584]{1,0:T(8,128)(2,1)}, bf16[64,3584]{1,0:T(8,128)(2,1)}, u32[]{:S(2)}, u32[]{:S(2)}) collective-permute-start(bf16[64,3584]{1,0:T(8,128)(2,1)} %slice.201), channel_id=1, source_target_pairs={{0,48},{16,0},{32,16},{48,32},{1,49},{17,1},{33,17},{49,33},{2,50}... | collective-permute-start | bytes 1376264 | tf_op jit(solution)/shard_map/ppermute | solution.py:14
  358.2 22.9 %collective-permute-start.16 = (bf16[64,3584]{1,0:T(8,128)(2,1)}, bf16[64,3584]{1,0:T(8,128)(2,1)}, u32[]{:S(2)}, u32[]{:S(2)}) collective-permute-start(bf16[64,3584]{1,0:T(8,128)(2,1)} %get-tuple-element.12), channel_id=1, source_target_pairs={{0,48},{16,0},{32,16},{48,32},{1,49},{17,1},{33,17},{49,33},{2,50}... | collective-permute-start | bytes 1376264 | tf_op jit(solution)/shard_map/ppermute | solution.py:14
  359.8 34.9 %collective-permute-start.15 = (bf16[64,3584]{1,0:T(8,128)(2,1)}, bf16[64,3584]{1,0:T(8,128)(2,1)S(1)}, u32[]{:S(2)}, u32[]{:S(2)}) collective-permute-start(bf16[64,3584]{1,0:T(8,128)(2,1)} %get-tuple-element.9), channel_id=1, source_target_pairs={{0,16},{16,32},{32,48},{48,0},{1,17},{17,33},{33,49},{49,1},{2,18}... | collective-permute-start | bytes 1376264 | tf_op jit(solution)/shard_map/ppermute | solution.py:14
  359.8 35.0 %collective-permute-start.19 = (bf16[64,3584]{1,0:T(8,128)(2,1)}, bf16[64,3584]{1,0:T(8,128)(2,1)}, u32[]{:S(2)}, u32[]{:S(2)}) collective-permute-start(bf16[64,3584]{1,0:T(8,128)(2,1)} %get-tuple-element.10), channel_id=1, source_target_pairs={{0,16},{16,32},{32,48},{48,0},{1,17},{17,33},{33,49},{49,1},{2,18}... | collective-permute-start | bytes 1376264 | tf_op jit(solution)/shard_map/ppermute | solution.py:14
  361.1 64.9 %collective-permute-start.18 = (bf16[64,3584]{1,0:T(8,128)(2,1)}, bf16[64,3584]{1,0:T(8,128)(2,1)}, u32[]{:S(2)}, u32[]{:S(2)}) collective-permute-start(bf16[64,3584]{1,0:T(8,128)(2,1)} %get-tuple-element.11), channel_id=1, source_target_pairs={{0,48},{16,0},{32,16},{48,32},{1,49},{17,1},{33,17},{49,33},{2,50}... | collective-permute-start | bytes 1376264 | tf_op jit(solution)/shard_map/ppermute | solution.py:14
  381.2 27.5 %collective-permute-start.37 = (bf16[64,3584]{1,0:T(8,128)(2,1)S(1)}, bf16[64,3584]{1,0:T(8,128)(2,1)S(1)}, u32[]{:S(2)}, u32[]{:S(2)}) collective-permute-start(bf16[64,3584]{1,0:T(8,128)(2,1)S(1)} %get-tuple-element.21), channel_id=1, source_target_pairs={{0,16},{16,32},{32,48},{48,0},{1,17},{17,33},{33,49},{49,1},{2,18}... | collective-permute-start | bytes 1376264 | tf_op jit(solution)/shard_map/ppermute | solution.py:14
  394.7 14.1 %collective-permute-start.41 = (bf16[64,3584]{1,0:T(8,128)(2,1)S(1)}, bf16[64,3584]{1,0:T(8,128)(2,1)S(1)}, u32[]{:S(2)}, u32[]{:S(2)}) collective-permute-start(bf16[64,3584]{1,0:T(8,128)(2,1)S(1)} %get-tuple-element.22), channel_id=1, source_target_pairs={{0,16},{16,32},{32,48},{48,0},{1,17},{17,33},{33,49},{49,1},{2,18}... | collective-permute-start | bytes 1376264 | tf_op jit(solution)/shard_map/ppermute | solution.py:14
  394.8 38.5 %collective-permute-start.40 = (bf16[64,3584]{1,0:T(8,128)(2,1)}, bf16[64,3584]{1,0:T(8,128)(2,1)}, u32[]{:S(2)}, u32[]{:S(2)}) collective-permute-start(bf16[64,3584]{1,0:T(8,128)(2,1)} %get-tuple-element.23), channel_id=1, source_target_pairs={{0,48},{16,0},{32,16},{48,32},{1,49},{17,1},{33,17},{49,33},{2,50}... | collective-permute-start | bytes 1376264 | tf_op jit(solution)/shard_map/ppermute | solution.py:14
  403.9 19.6 %collective-permute-start.39 = (bf16[64,3584]{1,0:T(8,128)(2,1)S(1)}, bf16[64,3584]{1,0:T(8,128)(2,1)S(1)}, u32[]{:S(2)}, u32[]{:S(2)}) collective-permute-start(bf16[64,3584]{1,0:T(8,128)(2,1)S(1)} %add_convert_fusion.3), channel_id=1, source_target_pairs={{0,48},{16,0},{32,16},{48,32},{1,49},{17,1},{33,17},{49,33},{2,50}... | collective-permute-start | bytes 1376264 | tf_op jit(solution)/shard_map/ppermute | solution.py:14
  408.7 17.4 %collective-permute-start.20 = (bf16[64,3584]{1,0:T(8,128)(2,1)S(1)}, bf16[64,3584]{1,0:T(8,128)(2,1)S(1)}, u32[]{:S(2)}, u32[]{:S(2)}) collective-permute-start(bf16[64,3584]{1,0:T(8,128)(2,1)S(1)} %get-tuple-element.8), channel_id=1, source_target_pairs={{0,16},{16,32},{32,48},{48,0},{1,17},{17,33},{33,49},{49,1},{2,18}... | collective-permute-start | bytes 1376264 | tf_op jit(solution)/shard_map/ppermute | solution.py:14
  425.9 14.2 %collective-permute-start.42 = (bf16[64,3584]{1,0:T(8,128)(2,1)}, bf16[64,3584]{1,0:T(8,128)(2,1)}, u32[]{:S(2)}, u32[]{:S(2)}) collective-permute-start(bf16[64,3584]{1,0:T(8,128)(2,1)} %get-tuple-element.20), channel_id=1, source_target_pairs={{0,16},{16,32},{32,48},{48,0},{1,17},{17,33},{33,49},{49,1},{2,18}... | collective-permute-start | bytes 1376264 | tf_op jit(solution)/shard_map/ppermute | solution.py:14
  428.3 30.6 %all-to-all-start.3 = ((bf16[16,8,3584]{2,1,0:T(8,128)(2,1)}), bf16[16,8,3584]{2,1,0:T(8,128)(2,1)}, u32[]{:S(2)}, u32[]{:S(2)}) async-start(bf16[16,8,3584]{2,1,0:T(8,128)(2,1)} %maximum_bitcast_fusion.1), calls=%async_computation.3 | async-start | bytes 1835008 | tf_op jit(solution)/shard_map/all_to_all | solution.py:87
  458.9 28.8 %all-to-all-start.7 = ((bf16[16,8,3584]{2,1,0:T(8,128)(2,1)}), bf16[16,8,3584]{2,1,0:T(8,128)(2,1)}, u32[]{:S(2)}, u32[]{:S(2)}) async-start(bf16[16,8,3584]{2,1,0:T(8,128)(2,1)} %maximum_bitcast_fusion.3), calls=%async_computation.7 | async-start | bytes 1835008 | tf_op jit(solution)/shard_map/all_to_all | solution.py:87
  466.2 24.3 %collective-permute-start.21 = (bf16[64,3584]{1,0:T(8,128)(2,1)}, bf16[64,3584]{1,0:T(8,128)(2,1)S(1)}, u32[]{:S(2)}, u32[]{:S(2)}) collective-permute-start(bf16[64,3584]{1,0:T(8,128)(2,1)} %fusion.9), channel_id=1, source_target_pairs={{0,64},{64,128},{128,192},{192,0},{1,65},{65,129},{129,193},{193,1... | collective-permute-start | bytes 1376264 | tf_op jit(solution)/shard_map/ppermute | solution.py:14
  (22 other events, 293.1 us)

commit v3 on v2

--- a/solution.py
+++ b/solution.py
@@ -32,7 +32,7 @@
         hidden = (jax.nn.silu(gate_proj) * up_proj).astype(jnp.bfloat16)
         return jnp.dot(hidden, down_mat, preferred_element_type=jnp.float32).astype(jnp.bfloat16)
 
-    def apply_layer(tokens_in, route_ids):
+    def prepare(tokens_in, route_ids):
         x_float = tokens_in.astype(jnp.float32)
         mean_sq = jnp.mean(x_float * x_float, axis=1, keepdims=True)
         normed = (x_float * lax.rsqrt(mean_sq + 1e-06) * gain_row[None, :]).astype(jnp.bfloat16)
@@ -49,6 +49,9 @@
         ).astype(jnp.bfloat16)
         outbox = jnp.dot(placing, normed, preferred_element_type=jnp.float32).astype(jnp.bfloat16)
         outbox = outbox.reshape(row_size, capacity, width)
+        return x_float, gate_val, placing, outbox
+
+    def gather_compute(outbox):
         arrived = lax.all_to_all(outbox, ROW, split_axis=0, concat_axis=0, tiled=True)
         own = arrived.reshape(-1, width)
         half = own.shape[0] // 2
@@ -57,9 +60,12 @@
         far_low = passed_along(from_below[:half], "y", 1)
         far_high = passed_along(from_above[half:], "y", -1)
         rows = jnp.concatenate([own, from_below, from_above, far_low, far_high], axis=0)
-        partial_out = expert_compute(rows)
+        return expert_compute(rows)
+
+    def scatter_back(partial_out, x_float, gate_val, placing):
+        half = partial_out.shape[0] // 8
         q_own, q_below, q_above, q_far_low, q_far_high = jnp.split(
-            partial_out, [own.shape[0], 2 * own.shape[0], 3 * own.shape[0], 3 * own.shape[0] + half]
+            partial_out, [2 * half, 4 * half, 6 * half, 7 * half]
         )
         back_below = passed_along(q_far_low, "y", -1)
         back_above = passed_along(q_far_high, "y", 1)
@@ -95,10 +101,16 @@
     micro_count = acts.shape[1]
     carried = [acts[0, micro_idx] for micro_idx in range(micro_count)]
     for round_idx in range(routes.shape[1]):
-        carried = [
-            passed_along(apply_layer(carried[micro_idx], routes[0, round_idx, micro_idx]), "section", 1)
-            for micro_idx in range(micro_count)
-        ]
+        updated = []
+        ahead = None
+        for micro_idx in range(micro_count):
+            x_float, gate_val, placing, outbox = prepare(carried[micro_idx], routes[0, round_idx, micro_idx])
+            if ahead is not None:
+                outbox, ahead_out = lax.optimization_barrier((outbox, ahead[0]))
+                updated.append(scatter_back(ahead_out, *ahead[1:]))
+            ahead = (gather_compute(outbox), x_float, gate_val, placing)
+        updated.append(scatter_back(*ahead))
+        carried = [passed_along(value, "section", 1) for value in updated]
     return jnp.stack(carried)[None]
 
 

time: 511 us -> 556 us (1.088)
  waiting for transfers between devices: 276 us -> 318 us
  local copies, waits for them, and re-layouts: 42 us -> 34.8 us
    ppermute x44, waiting for transfers between devices: 142 us -> 206 us  [passed_along(): return lax.ppermute(value, axis, pairs)]
    all_to_all x8, waiting for transfers between devices: 133 us -> 112 us  [the longest x4 73.2 us: gather_compute(): lax.all_to_all(outbox, ROW, split_axis=0, concat_axis=0, tiled=True)]
    all_to_all x8, starting transfers between devices: 41.2 us -> 51.4 us  [the longest x4 32.5 us: gather_compute(): lax.all_to_all(outbox, ROW, split_axis=0, concat_axis=0, tiled=True)]
    ppermute x44, starting transfers between devices: 59.9 us -> 52 us  [passed_along(): return lax.ppermute(value, axis, pairs)]
    slice x12, local copies, waits for them, and re-layouts: 18.1 us -> 11.8 us  [the longest x4 9.91 us: scatter_back(): direct_above = passed_along(q_above[:half], 'y', 1)]
    unnamed x52 -> x46, local copies, waits for them, and re-layouts: 20.3 us -> 19.7 us
  transfers between devices with their start and end apart: 52 -> 52, of which waited for: 24 -> 33; matrix products, arithmetic and copies ran while one was open for 22% -> 17% of each run, Pallas kernels for 0% -> 0%
where the time goes in v3:
time: 556 us; the launch traced here: 546 us
  waiting for transfers between devices  318 us (57%)
  starting transfers between devices  103 us (19%)
  matrix products  59 us (11%)
  local copies, waits for them, and re-layouts  34.8 us (6%)
  other arithmetic  29.7 us (5%)
    ppermute x44, waiting for transfers between devices, passed_along(): return lax.ppermute(value, axis, pairs)  206 us
    all_to_all x4, waiting for transfers between devices, gather_compute(): lax.all_to_all(outbox, ROW, split_axis=0, concat_axis=0, tiled=True)  73.2 us
    ppermute x44, starting transfers between devices, passed_along(): return lax.ppermute(value, axis, pairs)  52 us
    all_to_all x4, waiting for transfers between devices, scatter_back(): lax.all_to_all(summed.reshape(row_size, capacity, width), ROW, split_axis...  39.1 us
    dot_general x4, matrix products, expert_compute(): jnp.dot(hidden, down_mat, preferred_element_type=jnp.float32)  33.6 us
    all_to_all x4, starting transfers between devices, gather_compute(): lax.all_to_all(outbox, ROW, split_axis=0, concat_axis=0, tiled=True)  32.5 us
    unnamed x46, local copies, waits for them, and re-layouts  19.7 us
    all_to_all x4, starting transfers between devices, scatter_back(): lax.all_to_all(summed.reshape(row_size, capacity, width), ROW, split_axis...  18.9 us
  transfers between devices with their start and end apart: 52, of which 33 were waited for; matrix products, arithmetic and copies ran while one was open for 17% of the time, Pallas kernels for 0%

profile of v3, /device:TPU:1, one launch (start us, length us, event | category | flops | bytes accessed | tf_op | source)
XLA Modules:
  0.0 545.8 jit_solution(1448953437013178909)
XLA Ops:
  7.3 10.0 %all-to-all-start = ((bf16[16,8,3584]{2,1,0:T(8,128)(2,1)}), bf16[16,8,3584]{2,1,0:T(8,128)(2,1)}, u32[]{:S(2)}, u32[]{:S(2)}) async-start(bf16[16,8,3584]{2,1,0:T(8,128)(2,1)} %fusion.5), calls=%async_computation | async-start | bytes 1835008 | tf_op jit(solution)/shard_map/all_to_all | solution.py:55
  18.7 24.1 %all-to-all-done = bf16[16,8,3584]{2,1,0:T(8,128)(2,1)} async-done(((bf16[16,8,3584]{2,1,0:T(8,128)(2,1)}), bf16[16,8,3584]{2,1,0:T(8,128)(2,1)}, u32[]{:S(2)}, u32[]{:S(2)}) %all-to-all-start) | async-done | bytes 917536 | tf_op jit(solution)/shard_map/all_to_all | solution.py:55
  46.8 17.8 %collective-permute-done = bf16[128,3584]{1,0:T(8,128)(2,1)S(1)} collective-permute-done((bf16[128,3584]{1,0:T(8,128)(2,1)}, bf16[128,3584]{1,0:T(8,128)(2,1)S(1)}, u32[]{:S(2)}, u32[]{:S(2)}) %collective-permute-start) | collective-permute-done | bytes 917536 | tf_op jit(solution)/shard_map/ppermute | solution.py:14
  65.1 2.5 collective-permute-start.3
  67.8 9.8 %collective-permute-done.2 = bf16[64,3584]{1,0:T(8,128)(2,1)S(1)} collective-permute-done((bf16[64,3584]{1,0:T(8,128)(2,1)S(1)}, bf16[64,3584]{1,0:T(8,128)(2,1)S(1)}, u32[]{:S(2)}, u32[]{:S(2)}) %collective-permute-start.2) | collective-permute-done | bytes 458784 | tf_op jit(solution)/shard_map/ppermute | solution.py:14
  81.5 8.4 %convolution_convert_fusion.3 = bf16[512,3584]{1,0:T(8,128)(2,1)} fusion(bf16[1,1,256,3584]{3,2,1,0:T(8,128)(2,1)S(1)} %copy-done, f32[512,256]{1,0:T(8,128)} %fusion.22, bf16[512,3584]{1,0:T(8,128)(2,1)} %copy-done.7, bf16[1,1,3584,256]{3,2,1,0:T(8,128)(2,1)} %param.11), kind=kOutput, calls=%fused_computation.3 | convolution fusion | flops 1881669632 | bytes 11534336 | tf_op jit(solution)/shard_map/dot_general | solution.py:33
  92.2 3.1 collective-permute-start.5
  95.3 9.5 %collective-permute-done.5 = bf16[64,3584]{1,0:T(8,128)(2,1)S(1)} collective-permute-done((bf16[64,3584]{1,0:T(8,128)(2,1)S(1)}, bf16[64,3584]{1,0:T(8,128)(2,1)S(1)}, u32[]{:S(2)}, u32[]{:S(2)}) %collective-permute-start.5) | collective-permute-done | bytes 458784 | tf_op jit(solution)/shard_map/ppermute | solution.py:14
  106.0 3.5 collective-permute-start.6
  109.8 8.0 %collective-permute-done.8 = bf16[64,3584]{1,0:T(8,128)(2,1)S(1)} collective-permute-done((bf16[64,3584]{1,0:T(8,128)(2,1)S(1)}, bf16[64,3584]{1,0:T(8,128)(2,1)S(1)}, u32[]{:S(2)}, u32[]{:S(2)}) %collective-permute-start.8) | collective-permute-done | bytes 458784 | tf_op jit(solution)/shard_map/ppermute | solution.py:14
  120.3 7.8 %all-to-all-start.2 = ((bf16[16,8,3584]{2,1,0:T(8,128)(2,1)}), bf16[16,8,3584]{2,1,0:T(8,128)(2,1)}, u32[]{:S(2)}, u32[]{:S(2)}) async-start(bf16[16,8,3584]{2,1,0:T(8,128)(2,1)} %fusion.4), calls=%async_computation.2 | async-start | bytes 1835008 | tf_op jit(solution)/shard_map/all_to_all | solution.py:55
  128.5 2.6 collective-permute-done.9
  133.6 20.0 %all-to-all-done.2 = bf16[16,8,3584]{2,1,0:T(8,128)(2,1)} async-done(((bf16[16,8,3584]{2,1,0:T(8,128)(2,1)}), bf16[16,8,3584]{2,1,0:T(8,128)(2,1)}, u32[]{:S(2)}, u32[]{:S(2)}) %all-to-all-start.2) | async-done | bytes 917536 | tf_op jit(solution)/shard_map/all_to_all | solution.py:55
  153.6 4.2 all-to-all-start.1
  162.7 18.8 %collective-permute-done.11 = bf16[128,3584]{1,0:T(8,128)(2,1)S(1)} collective-permute-done((bf16[128,3584]{1,0:T(8,128)(2,1)}, bf16[128,3584]{1,0:T(8,128)(2,1)S(1)}, u32[]{:S(2)}, u32[]{:S(2)}) %collective-permute-start.11) | collective-permute-done | bytes 917536 | tf_op jit(solution)/shard_map/ppermute | solution.py:14
  184.8 10.1 %collective-permute-done.13 = bf16[64,3584]{1,0:T(8,128)(2,1)S(1)} collective-permute-done((bf16[64,3584]{1,0:T(8,128)(2,1)S(1)}, bf16[64,3584]{1,0:T(8,128)(2,1)S(1)}, u32[]{:S(2)}, u32[]{:S(2)}) %collective-permute-start.13) | collective-permute-done | bytes 458784 | tf_op jit(solution)/shard_map/ppermute | solution.py:14
  199.3 8.4 %convolution_convert_fusion.2 = bf16[512,3584]{1,0:T(8,128)(2,1)} fusion(bf16[1,1,256,3584]{3,2,1,0:T(8,128)(2,1)S(1)} %copy-done, f32[512,256]{1,0:T(8,128)} %fusion.20, bf16[512,3584]{1,0:T(8,128)(2,1)} %copy-done.8, bf16[1,1,3584,256]{3,2,1,0:T(8,128)(2,1)} %param.11), kind=kOutput, calls=%fused_computation.2 | convolution fusion | flops 1881669632 | bytes 11534336 | tf_op jit(solution)/shard_map/dot_general | solution.py:33
  207.7 2.7 fusion.125
  216.3 5.6 %collective-permute-done.16 = bf16[64,3584]{1,0:T(8,128)(2,1)} collective-permute-done((bf16[64,3584]{1,0:T(8,128)(2,1)}, bf16[64,3584]{1,0:T(8,128)(2,1)}, u32[]{:S(2)}, u32[]{:S(2)}) %collective-permute-start.16) | collective-permute-done | bytes 458784 | tf_op jit(solution)/shard_map/ppermute | solution.py:14
  223.1 3.2 collective-permute-start.17
  227.1 9.8 %collective-permute-done.19 = bf16[64,3584]{1,0:T(8,128)(2,1)S(1)} collective-permute-done((bf16[64,3584]{1,0:T(8,128)(2,1)}, bf16[64,3584]{1,0:T(8,128)(2,1)S(1)}, u32[]{:S(2)}, u32[]{:S(2)}) %collective-permute-start.19) | collective-permute-done | bytes 458784 | tf_op jit(solution)/shard_map/ppermute | solution.py:14
  240.7 7.6 %all-to-all-start.4 = ((bf16[16,8,3584]{2,1,0:T(8,128)(2,1)}), bf16[16,8,3584]{2,1,0:T(8,128)(2,1)}, u32[]{:S(2)}, u32[]{:S(2)}) async-start(bf16[16,8,3584]{2,1,0:T(8,128)(2,1)} %fusion.7), calls=%async_computation.4 | async-start | bytes 1835008 | tf_op jit(solution)/shard_map/all_to_all | solution.py:55
  253.3 20.5 %all-to-all-done.4 = bf16[16,8,3584]{2,1,0:T(8,128)(2,1)} async-done(((bf16[16,8,3584]{2,1,0:T(8,128)(2,1)}), bf16[16,8,3584]{2,1,0:T(8,128)(2,1)}, u32[]{:S(2)}, u32[]{:S(2)}) %all-to-all-start.4) | async-done | bytes 917536 | tf_op jit(solution)/shard_map/all_to_all | solution.py:55
  273.7 4.2 all-to-all-start.3
  284.0 17.9 %collective-permute-done.22 = bf16[128,3584]{1,0:T(8,128)(2,1)S(1)} collective-permute-done((bf16[128,3584]{1,0:T(8,128)(2,1)}, bf16[128,3584]{1,0:T(8,128)(2,1)S(1)}, u32[]{:S(2)}, u32[]{:S(2)}) %collective-permute-start.22) | collective-permute-done | bytes 917536 | tf_op jit(solution)/shard_map/ppermute | solution.py:14
  308.2 2.5 fusion.9
  320.9 3.9 fusion.18
  324.8 8.4 %convolution_convert_fusion.1 = bf16[512,3584]{1,0:T(8,128)(2,1)} fusion(bf16[1,1,256,3584]{3,2,1,0:T(8,128)(2,1)S(1)} %copy-done, f32[512,256]{1,0:T(8,128)} %fusion.18, bf16[512,3584]{1,0:T(8,128)(2,1)} %constant_dynamic-update-slice_fusion.10, bf16[1,1,3584,256]{3,2,1,0:T(8,128)(2,1)} %param.11), kind=kOutput, calls=%fused_computation.1 | convolution fusion | flops 1881669632 | bytes 11534336 | tf_op jit(solution)/shard_map/dot_general | solution.py:33
  334.9 7.1 %all-to-all-start.6 = ((bf16[16,8,3584]{2,1,0:T(8,128)(2,1)}), bf16[16,8,3584]{2,1,0:T(8,128)(2,1)}, u32[]{:S(2)}, u32[]{:S(2)}) async-start(bf16[16,8,3584]{2,1,0:T(8,128)(2,1)} %fusion.6), calls=%async_computation.6 | async-start | bytes 1835008 | tf_op jit(solution)/shard_map/all_to_all | solution.py:55
  342.0 2.6 fusion.122
  344.5 2.6 collective-permute-start.27
  347.2 2.7 collective-permute-start.29
  349.9 7.0 %collective-permute-done.27 = bf16[64,3584]{1,0:T(8,128)(2,1)S(1)} collective-permute-done((bf16[64,3584]{1,0:T(8,128)(2,1)S(1)}, bf16[64,3584]{1,0:T(8,128)(2,1)S(1)}, u32[]{:S(2)}, u32[]{:S(2)}) %collective-permute-start.27) | collective-permute-done | bytes 458784 | tf_op jit(solution)/shard_map/ppermute | solution.py:14
  358.8 8.7 %all-to-all-done.6 = bf16[16,8,3584]{2,1,0:T(8,128)(2,1)} async-done(((bf16[16,8,3584]{2,1,0:T(8,128)(2,1)}), bf16[16,8,3584]{2,1,0:T(8,128)(2,1)}, u32[]{:S(2)}, u32[]{:S(2)}) %all-to-all-start.6) | async-done | bytes 917536 | tf_op jit(solution)/shard_map/all_to_all | solution.py:55
  371.4 18.9 %collective-permute-done.33 = bf16[128,3584]{1,0:T(8,128)(2,1)S(1)} collective-permute-done((bf16[128,3584]{1,0:T(8,128)(2,1)}, bf16[128,3584]{1,0:T(8,128)(2,1)S(1)}, u32[]{:S(2)}, u32[]{:S(2)}) %collective-permute-start.33) | collective-permute-done | bytes 917536 | tf_op jit(solution)/shard_map/ppermute | solution.py:14
  392.1 12.6 %collective-permute-done.35 = bf16[64,3584]{1,0:T(8,128)(2,1)S(1)} collective-permute-done((bf16[64,3584]{1,0:T(8,128)(2,1)S(1)}, bf16[64,3584]{1,0:T(8,128)(2,1)S(1)}, u32[]{:S(2)}, u32[]{:S(2)}) %collective-permute-start.35) | collective-permute-done | bytes 458784 | tf_op jit(solution)/shard_map/ppermute | solution.py:14
  405.0 11.6 %collective-permute-done.36 = bf16[64,3584]{1,0:T(8,128)(2,1)S(1)} collective-permute-done((bf16[64,3584]{1,0:T(8,128)(2,1)S(1)}, bf16[64,3584]{1,0:T(8,128)(2,1)S(1)}, u32[]{:S(2)}, u32[]{:S(2)}) %collective-permute-start.36) | collective-permute-done | bytes 458784 | tf_op jit(solution)/shard_map/ppermute | solution.py:14
  420.4 8.4 %convolution_convert_fusion = bf16[512,3584]{1,0:T(8,128)(2,1)} fusion(bf16[1,1,256,3584]{3,2,1,0:T(8,128)(2,1)S(1)} %copy-done, f32[512,256]{1,0:T(8,128)} %fusion.16, bf16[512,3584]{1,0:T(8,128)(2,1)} %copy-done.9, bf16[1,1,3584,256]{3,2,1,0:T(8,128)(2,1)} %param.11), kind=kOutput, calls=%fused_computation | convolution fusion | flops 1881669632 | bytes 11534336 | tf_op jit(solution)/shard_map/dot_general | solution.py:33
  436.3 5.8 %collective-permute-done.38 = bf16[64,3584]{1,0:T(8,128)(2,1)S(1)} collective-permute-done((bf16[64,3584]{1,0:T(8,128)(2,1)S(1)}, bf16[64,3584]{1,0:T(8,128)(2,1)S(1)}, u32[]{:S(2)}, u32[]{:S(2)}) %collective-permute-start.38) | collective-permute-done | bytes 458784 | tf_op jit(solution)/shard_map/ppermute | solution.py:14
  443.2 3.1 collective-permute-start.39
  448.9 8.4 %collective-permute-done.37 = bf16[64,3584]{1,0:T(8,128)(2,1)S(1)} collective-permute-done((bf16[64,3584]{1,0:T(8,128)(2,1)S(1)}, bf16[64,3584]{1,0:T(8,128)(2,1)S(1)}, u32[]{:S(2)}, u32[]{:S(2)}) %collective-permute-start.37) | collective-permute-done | bytes 458784 | tf_op jit(solution)/shard_map/ppermute | solution.py:14
  457.3 9.8 %collective-permute-done.41 = bf16[64,3584]{1,0:T(8,128)(2,1)S(1)} collective-permute-done((bf16[64,3584]{1,0:T(8,128)(2,1)S(1)}, bf16[64,3584]{1,0:T(8,128)(2,1)S(1)}, u32[]{:S(2)}, u32[]{:S(2)}) %collective-permute-start.41) | collective-permute-done | bytes 458784 | tf_op jit(solution)/shard_map/ppermute | solution.py:14
  470.5 6.3 %all-to-all-start.5 = ((bf16[16,8,3584]{2,1,0:T(8,128)(2,1)}), bf16[16,8,3584]{2,1,0:T(8,128)(2,1)}, u32[]{:S(2)}, u32[]{:S(2)}) async-start(bf16[16,8,3584]{2,1,0:T(8,128)(2,1)} %maximum_bitcast_fusion.2), calls=%async_computation.5 | async-start | bytes 1835008 | tf_op jit(solution)/shard_map/all_to_all | solution.py:93
  476.7 4.2 collective-permute-done.42
  483.4 18.8 %all-to-all-done.5 = bf16[16,8,3584]{2,1,0:T(8,128)(2,1)} async-done(((bf16[16,8,3584]{2,1,0:T(8,128)(2,1)}), bf16[16,8,3584]{2,1,0:T(8,128)(2,1)}, u32[]{:S(2)}, u32[]{:S(2)}) %all-to-all-start.5) | async-done | bytes 917536 | tf_op jit(solution)/shard_map/all_to_all | solution.py:93
  502.2 4.2 all-to-all-start.7
  510.7 20.2 %all-to-all-done.7 = bf16[16,8,3584]{2,1,0:T(8,128)(2,1)} async-done(((bf16[16,8,3584]{2,1,0:T(8,128)(2,1)}), bf16[16,8,3584]{2,1,0:T(8,128)(2,1)}, u32[]{:S(2)}, u32[]{:S(2)}) %all-to-all-start.7) | async-done | bytes 917536 | tf_op jit(solution)/shard_map/all_to_all | solution.py:93
  533.7 10.7 %collective-permute-done.43 = bf16[64,3584]{1,0:T(8,128)(2,1)S(1)} collective-permute-done((bf16[64,3584]{1,0:T(8,128)(2,1)S(1)}, bf16[64,3584]{1,0:T(8,128)(2,1)S(1)}, u32[]{:S(2)}, u32[]{:S(2)}) %collective-permute-start.43) | collective-permute-done | bytes 458784 | tf_op jit(solution)/shard_map/ppermute | solution.py:14
  (187 shorter events, 116.3 us)
Async XLA Ops:
  7.3 35.4 %all-to-all-start = ((bf16[16,8,3584]{2,1,0:T(8,128)(2,1)}), bf16[16,8,3584]{2,1,0:T(8,128)(2,1)}, u32[]{:S(2)}, u32[]{:S(2)}) async-start(bf16[16,8,3584]{2,1,0:T(8,128)(2,1)} %fusion.5), calls=%async_computation | async-start | bytes 1835008 | tf_op jit(solution)/shard_map/all_to_all | solution.py:55
  42.7 21.8 %collective-permute-start = (bf16[128,3584]{1,0:T(8,128)(2,1)}, bf16[128,3584]{1,0:T(8,128)(2,1)S(1)}, u32[]{:S(2)}, u32[]{:S(2)}) collective-permute-start(bf16[128,3584]{1,0:T(8,128)(2,1)} %bitcast.8), channel_id=1, source_target_pairs={{0,16},{16,32},{32,48},{48,0},{1,17},{17,33},{33,49},{49,1},{2,18}... | collective-permute-start | bytes 2752520 | tf_op jit(solution)/shard_map/ppermute | solution.py:14
  44.0 21.0 %collective-permute-start.1 = (bf16[128,3584]{1,0:T(8,128)(2,1)}, bf16[128,3584]{1,0:T(8,128)(2,1)S(1)}, u32[]{:S(2)}, u32[]{:S(2)}) collective-permute-start(bf16[128,3584]{1,0:T(8,128)(2,1)} %bitcast.8), channel_id=1, source_target_pairs={{0,48},{16,0},{32,16},{48,32},{1,49},{17,1},{33,17},{49,33},{2,50}... | collective-permute-start | bytes 2752520 | tf_op jit(solution)/shard_map/ppermute | solution.py:14
  64.6 13.0 %collective-permute-start.2 = (bf16[64,3584]{1,0:T(8,128)(2,1)S(1)}, bf16[64,3584]{1,0:T(8,128)(2,1)S(1)}, u32[]{:S(2)}, u32[]{:S(2)}) collective-permute-start(bf16[64,3584]{1,0:T(8,128)(2,1)S(1)} %slice.176), channel_id=1, source_target_pairs={{0,16},{16,32},{32,48},{48,0},{1,17},{17,33},{33,49},{49,1},{2,18}... | collective-permute-start | bytes 1376264 | tf_op jit(solution)/shard_map/ppermute | solution.py:14
  65.1 12.6 %collective-permute-start.3 = (bf16[64,3584]{1,0:T(8,128)(2,1)S(1)}, bf16[64,3584]{1,0:T(8,128)(2,1)S(1)}, u32[]{:S(2)}, u32[]{:S(2)}) collective-permute-start(bf16[64,3584]{1,0:T(8,128)(2,1)S(1)} %slice.177), channel_id=1, source_target_pairs={{0,48},{16,0},{32,16},{48,32},{1,49},{17,1},{33,17},{49,33},{2,50}... | collective-permute-start | bytes 1376264 | tf_op jit(solution)/shard_map/ppermute | solution.py:14
  92.2 12.6 %collective-permute-start.5 = (bf16[64,3584]{1,0:T(8,128)(2,1)S(1)}, bf16[64,3584]{1,0:T(8,128)(2,1)S(1)}, u32[]{:S(2)}, u32[]{:S(2)}) collective-permute-start(bf16[64,3584]{1,0:T(8,128)(2,1)S(1)} %get-tuple-element.32), channel_id=1, source_target_pairs={{0,48},{16,0},{32,16},{48,32},{1,49},{17,1},{33,17},{49,33},{2,50}... | collective-permute-start | bytes 1376264 | tf_op jit(solution)/shard_map/ppermute | solution.py:14
  95.3 14.4 %collective-permute-start.4 = (bf16[64,3584]{1,0:T(8,128)(2,1)S(1)}, bf16[64,3584]{1,0:T(8,128)(2,1)S(1)}, u32[]{:S(2)}, u32[]{:S(2)}) collective-permute-start(bf16[64,3584]{1,0:T(8,128)(2,1)S(1)} %get-tuple-element.29), channel_id=1, source_target_pairs={{0,16},{16,32},{32,48},{48,0},{1,17},{17,33},{33,49},{49,1},{2,18}... | collective-permute-start | bytes 1376264 | tf_op jit(solution)/shard_map/ppermute | solution.py:14
  95.3 22.4 %collective-permute-start.8 = (bf16[64,3584]{1,0:T(8,128)(2,1)S(1)}, bf16[64,3584]{1,0:T(8,128)(2,1)S(1)}, u32[]{:S(2)}, u32[]{:S(2)}) collective-permute-start(bf16[64,3584]{1,0:T(8,128)(2,1)S(1)} %get-tuple-element.30), channel_id=1, source_target_pairs={{0,16},{16,32},{32,48},{48,0},{1,17},{17,33},{33,49},{49,1},{2,18}... | collective-permute-start | bytes 1376264 | tf_op jit(solution)/shard_map/ppermute | solution.py:14
  106.0 12.1 %collective-permute-start.6 = (bf16[64,3584]{1,0:T(8,128)(2,1)S(1)}, bf16[64,3584]{1,0:T(8,128)(2,1)S(1)}, u32[]{:S(2)}, u32[]{:S(2)}) collective-permute-start(bf16[64,3584]{1,0:T(8,128)(2,1)S(1)} %add_convert_fusion.15), channel_id=1, source_target_pairs={{0,48},{16,0},{32,16},{48,32},{1,49},{17,1},{33,17},{49,33},{2,50}... | collective-permute-start | bytes 1376264 | tf_op jit(solution)/shard_map/ppermute | solution.py:14
  109.4 19.0 %collective-permute-start.7 = (bf16[64,3584]{1,0:T(8,128)(2,1)}, bf16[64,3584]{1,0:T(8,128)(2,1)}, u32[]{:S(2)}, u32[]{:S(2)}) collective-permute-start(bf16[64,3584]{1,0:T(8,128)(2,1)} %get-tuple-element.31), channel_id=1, source_target_pairs={{0,48},{16,0},{32,16},{48,32},{1,49},{17,1},{33,17},{49,33},{2,50}... | collective-permute-start | bytes 1376264 | tf_op jit(solution)/shard_map/ppermute | solution.py:14
  120.3 33.4 %all-to-all-start.2 = ((bf16[16,8,3584]{2,1,0:T(8,128)(2,1)}), bf16[16,8,3584]{2,1,0:T(8,128)(2,1)}, u32[]{:S(2)}, u32[]{:S(2)}) async-start(bf16[16,8,3584]{2,1,0:T(8,128)(2,1)} %fusion.4), calls=%async_computation.2 | async-start | bytes 1835008 | tf_op jit(solution)/shard_map/all_to_all | solution.py:55
  153.6 58.9 %all-to-all-start.1 = ((bf16[16,8,3584]{2,1,0:T(8,128)(2,1)}), bf16[16,8,3584]{2,1,0:T(8,128)(2,1)}, u32[]{:S(2)}, u32[]{:S(2)}) async-start(bf16[16,8,3584]{2,1,0:T(8,128)(2,1)} %maximum_bitcast_fusion), calls=%async_computation.1 | async-start | bytes 1835008 | tf_op jit(solution)/shard_map/all_to_all | solution.py:93
  157.9 23.7 %collective-permute-start.11 = (bf16[128,3584]{1,0:T(8,128)(2,1)}, bf16[128,3584]{1,0:T(8,128)(2,1)S(1)}, u32[]{:S(2)}, u32[]{:S(2)}) collective-permute-start(bf16[128,3584]{1,0:T(8,128)(2,1)} %bitcast.17), channel_id=1, source_target_pairs={{0,16},{16,32},{32,48},{48,0},{1,17},{17,33},{33,49},{49,1},{2,18}... | collective-permute-start | bytes 2752520 | tf_op jit(solution)/shard_map/ppermute | solution.py:14
  159.5 23.5 %collective-permute-start.12 = (bf16[128,3584]{1,0:T(8,128)(2,1)}, bf16[128,3584]{1,0:T(8,128)(2,1)S(1)}, u32[]{:S(2)}, u32[]{:S(2)}) collective-permute-start(bf16[128,3584]{1,0:T(8,128)(2,1)} %bitcast.17), channel_id=1, source_target_pairs={{0,48},{16,0},{32,16},{48,32},{1,49},{17,1},{33,17},{49,33},{2,50}... | collective-permute-start | bytes 2752520 | tf_op jit(solution)/shard_map/ppermute | solution.py:14
  181.6 13.3 %collective-permute-start.13 = (bf16[64,3584]{1,0:T(8,128)(2,1)S(1)}, bf16[64,3584]{1,0:T(8,128)(2,1)S(1)}, u32[]{:S(2)}, u32[]{:S(2)}) collective-permute-start(bf16[64,3584]{1,0:T(8,128)(2,1)S(1)} %slice.178), channel_id=1, source_target_pairs={{0,16},{16,32},{32,48},{48,0},{1,17},{17,33},{33,49},{49,1},{2,18}... | collective-permute-start | bytes 1376264 | tf_op jit(solution)/shard_map/ppermute | solution.py:14
  183.0 12.5 %collective-permute-start.14 = (bf16[64,3584]{1,0:T(8,128)(2,1)S(1)}, bf16[64,3584]{1,0:T(8,128)(2,1)S(1)}, u32[]{:S(2)}, u32[]{:S(2)}) collective-permute-start(bf16[64,3584]{1,0:T(8,128)(2,1)S(1)} %slice.179), channel_id=1, source_target_pairs={{0,48},{16,0},{32,16},{48,32},{1,49},{17,1},{33,17},{49,33},{2,50}... | collective-permute-start | bytes 1376264 | tf_op jit(solution)/shard_map/ppermute | solution.py:14
  214.0 12.3 %collective-permute-start.10 = (bf16[64,3584]{1,0:T(8,128)(2,1)S(1)}, bf16[64,3584]{1,0:T(8,128)(2,1)S(1)}, u32[]{:S(2)}, u32[]{:S(2)}) collective-permute-start(bf16[64,3584]{1,0:T(8,128)(2,1)S(1)} %fusion.8), channel_id=1, source_target_pairs={{0,64},{64,128},{128,192},{192,0},{1,65},{65,129},{129,193},{193,1... | collective-permute-start | bytes 1376264 | tf_op jit(solution)/shard_map/ppermute | solution.py:14
  215.3 11.7 %collective-permute-start.15 = (bf16[64,3584]{1,0:T(8,128)(2,1)}, bf16[64,3584]{1,0:T(8,128)(2,1)S(1)}, u32[]{:S(2)}, u32[]{:S(2)}) collective-permute-start(bf16[64,3584]{1,0:T(8,128)(2,1)} %get-tuple-element.35), channel_id=1, source_target_pairs={{0,16},{16,32},{32,48},{48,0},{1,17},{17,33},{33,49},{49,1},{2,18}... | collective-permute-start | bytes 1376264 | tf_op jit(solution)/shard_map/ppermute | solution.py:14
  215.3 21.6 %collective-permute-start.19 = (bf16[64,3584]{1,0:T(8,128)(2,1)}, bf16[64,3584]{1,0:T(8,128)(2,1)S(1)}, u32[]{:S(2)}, u32[]{:S(2)}) collective-permute-start(bf16[64,3584]{1,0:T(8,128)(2,1)} %get-tuple-element.36), channel_id=1, source_target_pairs={{0,16},{16,32},{32,48},{48,0},{1,17},{17,33},{33,49},{49,1},{2,18}... | collective-permute-start | bytes 1376264 | tf_op jit(solution)/shard_map/ppermute | solution.py:14
  223.1 13.8 %collective-permute-start.17 = (bf16[64,3584]{1,0:T(8,128)(2,1)S(1)}, bf16[64,3584]{1,0:T(8,128)(2,1)S(1)}, u32[]{:S(2)}, u32[]{:S(2)}) collective-permute-start(bf16[64,3584]{1,0:T(8,128)(2,1)S(1)} %add_convert_fusion.11), channel_id=1, source_target_pairs={{0,48},{16,0},{32,16},{48,32},{1,49},{17,1},{33,17},{49,33},{2,50}... | collective-permute-start | bytes 1376264 | tf_op jit(solution)/shard_map/ppermute | solution.py:14
  226.3 22.0 %collective-permute-start.18 = (bf16[64,3584]{1,0:T(8,128)(2,1)}, bf16[64,3584]{1,0:T(8,128)(2,1)}, u32[]{:S(2)}, u32[]{:S(2)}) collective-permute-start(bf16[64,3584]{1,0:T(8,128)(2,1)} %get-tuple-element.37), channel_id=1, source_target_pairs={{0,48},{16,0},{32,16},{48,32},{1,49},{17,1},{33,17},{49,33},{2,50}... | collective-permute-start | bytes 1376264 | tf_op jit(solution)/shard_map/ppermute | solution.py:14
  240.7 33.1 %all-to-all-start.4 = ((bf16[16,8,3584]{2,1,0:T(8,128)(2,1)}), bf16[16,8,3584]{2,1,0:T(8,128)(2,1)}, u32[]{:S(2)}, u32[]{:S(2)}) async-start(bf16[16,8,3584]{2,1,0:T(8,128)(2,1)} %fusion.7), calls=%async_computation.4 | async-start | bytes 1835008 | tf_op jit(solution)/shard_map/all_to_all | solution.py:55
  273.7 34.5 %all-to-all-start.3 = ((bf16[16,8,3584]{2,1,0:T(8,128)(2,1)}), bf16[16,8,3584]{2,1,0:T(8,128)(2,1)}, u32[]{:S(2)}, u32[]{:S(2)}) async-start(bf16[16,8,3584]{2,1,0:T(8,128)(2,1)} %maximum_bitcast_fusion.1), calls=%async_computation.3 | async-start | bytes 1835008 | tf_op jit(solution)/shard_map/all_to_all | solution.py:93
  278.3 23.7 %collective-permute-start.22 = (bf16[128,3584]{1,0:T(8,128)(2,1)}, bf16[128,3584]{1,0:T(8,128)(2,1)S(1)}, u32[]{:S(2)}, u32[]{:S(2)}) collective-permute-start(bf16[128,3584]{1,0:T(8,128)(2,1)} %bitcast.22), channel_id=1, source_target_pairs={{0,16},{16,32},{32,48},{48,0},{1,17},{17,33},{33,49},{49,1},{2,18}... | collective-permute-start | bytes 2752520 | tf_op jit(solution)/shard_map/ppermute | solution.py:14
  279.9 24.9 %collective-permute-start.23 = (bf16[128,3584]{1,0:T(8,128)(2,1)}, bf16[128,3584]{1,0:T(8,128)(2,1)S(1)}, u32[]{:S(2)}, u32[]{:S(2)}) collective-permute-start(bf16[128,3584]{1,0:T(8,128)(2,1)} %bitcast.22), channel_id=1, source_target_pairs={{0,48},{16,0},{32,16},{48,32},{1,49},{17,1},{33,17},{49,33},{2,50}... | collective-permute-start | bytes 2752520 | tf_op jit(solution)/shard_map/ppermute | solution.py:14
  303.7 13.6 %collective-permute-start.24 = (bf16[64,3584]{1,0:T(8,128)(2,1)}, bf16[64,3584]{1,0:T(8,128)(2,1)}, u32[]{:S(2)}, u32[]{:S(2)}) collective-permute-start(bf16[64,3584]{1,0:T(8,128)(2,1)} %slice.186), channel_id=1, source_target_pairs={{0,16},{16,32},{32,48},{48,0},{1,17},{17,33},{33,49},{49,1},{2,18}... | collective-permute-start | bytes 1376264 | tf_op jit(solution)/shard_map/ppermute | solution.py:14
  306.6 12.5 %collective-permute-start.25 = (bf16[64,3584]{1,0:T(8,128)(2,1)}, bf16[64,3584]{1,0:T(8,128)(2,1)}, u32[]{:S(2)}, u32[]{:S(2)}) collective-permute-start(bf16[64,3584]{1,0:T(8,128)(2,1)} %slice.187), channel_id=1, source_target_pairs={{0,48},{16,0},{32,16},{48,32},{1,49},{17,1},{33,17},{49,33},{2,50}... | collective-permute-start | bytes 1376264 | tf_op jit(solution)/shard_map/ppermute | solution.py:14
  310.7 22.6 %collective-permute-start.21 = (bf16[64,3584]{1,0:T(8,128)(2,1)}, bf16[64,3584]{1,0:T(8,128)(2,1)S(1)}, u32[]{:S(2)}, u32[]{:S(2)}) collective-permute-start(bf16[64,3584]{1,0:T(8,128)(2,1)} %fusion.9), channel_id=1, source_target_pairs={{0,64},{64,128},{128,192},{192,0},{1,65},{65,129},{129,193},{193,1... | collective-permute-start | bytes 1376264 | tf_op jit(solution)/shard_map/ppermute | solution.py:14
  334.9 32.6 %all-to-all-start.6 = ((bf16[16,8,3584]{2,1,0:T(8,128)(2,1)}), bf16[16,8,3584]{2,1,0:T(8,128)(2,1)}, u32[]{:S(2)}, u32[]{:S(2)}) async-start(bf16[16,8,3584]{2,1,0:T(8,128)(2,1)} %fusion.6), calls=%async_computation.6 | async-start | bytes 1835008 | tf_op jit(solution)/shard_map/all_to_all | solution.py:55
  344.5 12.4 %collective-permute-start.27 = (bf16[64,3584]{1,0:T(8,128)(2,1)S(1)}, bf16[64,3584]{1,0:T(8,128)(2,1)S(1)}, u32[]{:S(2)}, u32[]{:S(2)}) collective-permute-start(bf16[64,3584]{1,0:T(8,128)(2,1)S(1)} %get-tuple-element.20), channel_id=1, source_target_pairs={{0,48},{16,0},{32,16},{48,32},{1,49},{17,1},{33,17},{49,33},{2,50}... | collective-permute-start | bytes 1376264 | tf_op jit(solution)/shard_map/ppermute | solution.py:14
  347.2 85.5 %collective-permute-start.26 = (bf16[64,3584]{1,0:T(8,128)(2,1)}, bf16[64,3584]{1,0:T(8,128)(2,1)S(1)}, u32[]{:S(2)}, u32[]{:S(2)}) collective-permute-start(bf16[64,3584]{1,0:T(8,128)(2,1)} %get-tuple-element.17), channel_id=1, source_target_pairs={{0,16},{16,32},{32,48},{48,0},{1,17},{17,33},{33,49},{49,1},{2,18}... | collective-permute-start | bytes 1376264 | tf_op jit(solution)/shard_map/ppermute | solution.py:14
  347.2 85.5 %collective-permute-start.30 = (bf16[64,3584]{1,0:T(8,128)(2,1)}, bf16[64,3584]{1,0:T(8,128)(2,1)}, u32[]{:S(2)}, u32[]{:S(2)}) collective-permute-start(bf16[64,3584]{1,0:T(8,128)(2,1)} %get-tuple-element.18), channel_id=1, source_target_pairs={{0,16},{16,32},{32,48},{48,0},{1,17},{17,33},{33,49},{49,1},{2,18}... | collective-permute-start | bytes 1376264 | tf_op jit(solution)/shard_map/ppermute | solution.py:14
  347.2 99.0 %collective-permute-start.29 = (bf16[64,3584]{1,0:T(8,128)(2,1)}, bf16[64,3584]{1,0:T(8,128)(2,1)}, u32[]{:S(2)}, u32[]{:S(2)}) collective-permute-start(bf16[64,3584]{1,0:T(8,128)(2,1)} %get-tuple-element.19), channel_id=1, source_target_pairs={{0,48},{16,0},{32,16},{48,32},{1,49},{17,1},{33,17},{49,33},{2,50}... | collective-permute-start | bytes 1376264 | tf_op jit(solution)/shard_map/ppermute | solution.py:14
  367.5 22.9 %collective-permute-start.33 = (bf16[128,3584]{1,0:T(8,128)(2,1)}, bf16[128,3584]{1,0:T(8,128)(2,1)S(1)}, u32[]{:S(2)}, u32[]{:S(2)}) collective-permute-start(bf16[128,3584]{1,0:T(8,128)(2,1)} %bitcast.26), channel_id=1, source_target_pairs={{0,16},{16,32},{32,48},{48,0},{1,17},{17,33},{33,49},{49,1},{2,18}... | collective-permute-start | bytes 2752520 | tf_op jit(solution)/shard_map/ppermute | solution.py:14
  368.5 22.6 %collective-permute-start.34 = (bf16[128,3584]{1,0:T(8,128)(2,1)}, bf16[128,3584]{1,0:T(8,128)(2,1)S(1)}, u32[]{:S(2)}, u32[]{:S(2)}) collective-permute-start(bf16[128,3584]{1,0:T(8,128)(2,1)} %bitcast.26), channel_id=1, source_target_pairs={{0,48},{16,0},{32,16},{48,32},{1,49},{17,1},{33,17},{49,33},{2,50}... | collective-permute-start | bytes 2752520 | tf_op jit(solution)/shard_map/ppermute | solution.py:14
  390.3 43.1 %collective-permute-start.28 = (bf16[64,3584]{1,0:T(8,128)(2,1)}, bf16[64,3584]{1,0:T(8,128)(2,1)}, u32[]{:S(2)}, u32[]{:S(2)}) collective-permute-start(bf16[64,3584]{1,0:T(8,128)(2,1)} %add_convert_fusion.7), channel_id=1, source_target_pairs={{0,48},{16,0},{32,16},{48,32},{1,49},{17,1},{33,17},{49,33},{2,50}... | collective-permute-start | bytes 1376264 | tf_op jit(solution)/shard_map/ppermute | solution.py:14
  391.1 13.6 %collective-permute-start.35 = (bf16[64,3584]{1,0:T(8,128)(2,1)S(1)}, bf16[64,3584]{1,0:T(8,128)(2,1)S(1)}, u32[]{:S(2)}, u32[]{:S(2)}) collective-permute-start(bf16[64,3584]{1,0:T(8,128)(2,1)S(1)} %slice.188), channel_id=1, source_target_pairs={{0,16},{16,32},{32,48},{48,0},{1,17},{17,33},{33,49},{49,1},{2,18}... | collective-permute-start | bytes 1376264 | tf_op jit(solution)/shard_map/ppermute | solution.py:14
  404.7 11.9 %collective-permute-start.36 = (bf16[64,3584]{1,0:T(8,128)(2,1)S(1)}, bf16[64,3584]{1,0:T(8,128)(2,1)S(1)}, u32[]{:S(2)}, u32[]{:S(2)}) collective-permute-start(bf16[64,3584]{1,0:T(8,128)(2,1)S(1)} %slice.189), channel_id=1, source_target_pairs={{0,48},{16,0},{32,16},{48,32},{1,49},{17,1},{33,17},{49,33},{2,50}... | collective-permute-start | bytes 1376264 | tf_op jit(solution)/shard_map/ppermute | solution.py:14
  435.3 12.1 %collective-permute-start.31 = (bf16[64,3584]{1,0:T(8,128)(2,1)S(1)}, bf16[64,3584]{1,0:T(8,128)(2,1)S(1)}, u32[]{:S(2)}, u32[]{:S(2)}) collective-permute-start(bf16[64,3584]{1,0:T(8,128)(2,1)S(1)} %get-tuple-element.16), channel_id=1, source_target_pairs={{0,16},{16,32},{32,48},{48,0},{1,17},{17,33},{33,49},{49,1},{2,18}... | collective-permute-start | bytes 1376264 | tf_op jit(solution)/shard_map/ppermute | solution.py:14
  435.4 21.9 %collective-permute-start.37 = (bf16[64,3584]{1,0:T(8,128)(2,1)S(1)}, bf16[64,3584]{1,0:T(8,128)(2,1)S(1)}, u32[]{:S(2)}, u32[]{:S(2)}) collective-permute-start(bf16[64,3584]{1,0:T(8,128)(2,1)S(1)} %get-tuple-element.23), channel_id=1, source_target_pairs={{0,16},{16,32},{32,48},{48,0},{1,17},{17,33},{33,49},{49,1},{2,18}... | collective-permute-start | bytes 1376264 | tf_op jit(solution)/shard_map/ppermute | solution.py:14
  435.5 31.6 %collective-permute-start.41 = (bf16[64,3584]{1,0:T(8,128)(2,1)S(1)}, bf16[64,3584]{1,0:T(8,128)(2,1)S(1)}, u32[]{:S(2)}, u32[]{:S(2)}) collective-permute-start(bf16[64,3584]{1,0:T(8,128)(2,1)S(1)} %get-tuple-element.24), channel_id=1, source_target_pairs={{0,16},{16,32},{32,48},{48,0},{1,17},{17,33},{33,49},{49,1},{2,18}... | collective-permute-start | bytes 1376264 | tf_op jit(solution)/shard_map/ppermute | solution.py:14
  443.2 23.9 %collective-permute-start.39 = (bf16[64,3584]{1,0:T(8,128)(2,1)S(1)}, bf16[64,3584]{1,0:T(8,128)(2,1)S(1)}, u32[]{:S(2)}, u32[]{:S(2)}) collective-permute-start(bf16[64,3584]{1,0:T(8,128)(2,1)S(1)} %add_convert_fusion.3), channel_id=1, source_target_pairs={{0,48},{16,0},{32,16},{48,32},{1,49},{17,1},{33,17},{49,33},{2,50}... | collective-permute-start | bytes 1376264 | tf_op jit(solution)/shard_map/ppermute | solution.py:14
  448.8 28.0 %collective-permute-start.40 = (bf16[64,3584]{1,0:T(8,128)(2,1)}, bf16[64,3584]{1,0:T(8,128)(2,1)}, u32[]{:S(2)}, u32[]{:S(2)}) collective-permute-start(bf16[64,3584]{1,0:T(8,128)(2,1)} %get-tuple-element.25), channel_id=1, source_target_pairs={{0,48},{16,0},{32,16},{48,32},{1,49},{17,1},{33,17},{49,33},{2,50}... | collective-permute-start | bytes 1376264 | tf_op jit(solution)/shard_map/ppermute | solution.py:14
  469.5 11.5 %collective-permute-start.42 = (bf16[64,3584]{1,0:T(8,128)(2,1)}, bf16[64,3584]{1,0:T(8,128)(2,1)}, u32[]{:S(2)}, u32[]{:S(2)}) collective-permute-start(bf16[64,3584]{1,0:T(8,128)(2,1)} %get-tuple-element.22), channel_id=1, source_target_pairs={{0,16},{16,32},{32,48},{48,0},{1,17},{17,33},{33,49},{49,1},{2,18}... | collective-permute-start | bytes 1376264 | tf_op jit(solution)/shard_map/ppermute | solution.py:14
  470.5 31.8 %all-to-all-start.5 = ((bf16[16,8,3584]{2,1,0:T(8,128)(2,1)}), bf16[16,8,3584]{2,1,0:T(8,128)(2,1)}, u32[]{:S(2)}, u32[]{:S(2)}) async-start(bf16[16,8,3584]{2,1,0:T(8,128)(2,1)} %maximum_bitcast_fusion.2), calls=%async_computation.5 | async-start | bytes 1835008 | tf_op jit(solution)/shard_map/all_to_all | solution.py:93
  502.2 28.7 %all-to-all-start.7 = ((bf16[16,8,3584]{2,1,0:T(8,128)(2,1)}), bf16[16,8,3584]{2,1,0:T(8,128)(2,1)}, u32[]{:S(2)}, u32[]{:S(2)}) async-start(bf16[16,8,3584]{2,1,0:T(8,128)(2,1)} %maximum_bitcast_fusion.3), calls=%async_computation.7 | async-start | bytes 1835008 | tf_op jit(solution)/shard_map/all_to_all | solution.py:93
  509.5 24.2 %collective-permute-start.32 = (bf16[64,3584]{1,0:T(8,128)(2,1)}, bf16[64,3584]{1,0:T(8,128)(2,1)S(1)}, u32[]{:S(2)}, u32[]{:S(2)}) collective-permute-start(bf16[64,3584]{1,0:T(8,128)(2,1)} %fusion.10), channel_id=1, source_target_pairs={{0,64},{64,128},{128,192},{192,0},{1,65},{65,129},{129,193},{193,1... | collective-permute-start | bytes 1376264 | tf_op jit(solution)/shard_map/ppermute | solution.py:14
  532.4 12.0 %collective-permute-start.43 = (bf16[64,3584]{1,0:T(8,128)(2,1)S(1)}, bf16[64,3584]{1,0:T(8,128)(2,1)S(1)}, u32[]{:S(2)}, u32[]{:S(2)}) collective-permute-start(bf16[64,3584]{1,0:T(8,128)(2,1)S(1)} %fusion.11), channel_id=1, source_target_pairs={{0,64},{64,128},{128,192},{192,0},{1,65},{65,129},{129,193},{193,1... | collective-permute-start | bytes 1376264 | tf_op jit(solution)/shard_map/ppermute | solution.py:14
  (19 other events, 331.8 us)
